TPU v7x, 256 devices: a whole 4x4x8 slice. The times are simulated.
256 devices in a mesh: view: 16 (over z, y_hi), row: 16 (over x, y_lo, core).
Axes of the slice: x: 4, y: 4 (y_hi: 2, y_lo: 2; y = y_hi * 2 + y_lo), z: 8, core: 2. Of those that a mesh axis runs over, the one named last changes fastest.
Arguments:
- latent: bfloat16 [1, 16, 32, 72, 1280], P(None, 'view', 'row'), may hold values from -30 to 30
- gn_gain: float32 [1280], replicated, may hold values from 0.25 to 1.75
- gn_bias: float32 [1280], replicated, may hold values from -3 to 3
- cam_idx: int32 [1, 16], P(None, 'view'), may hold values from 0 to 63
- noise_idx: int32 [1], replicated, may hold values from 0 to 999
- cam_table: bfloat16 [64, 2560], replicated, may hold values from -2 to 2
- noise_table: bfloat16 [1000, 2560], replicated, may hold values from -2 to 2
- conv_w: bfloat16 [3, 3, 1280, 1280], P(None, None, None, 'row'), may hold values from -0.0546875 to 0.0546875
- conv_bias: float32 [1280], replicated, may hold values from -3 to 3
- ln_gain: float32 [1280], replicated, may hold values from 0.25 to 1.75
- attn_in: bfloat16 [3, 1280, 1280], P(None, None, 'view'), may hold values from -0.15625 to 0.15625
- attn_out: bfloat16 [1280, 1280], P('view'), may hold values from -0.15625 to 0.15625
- head_scale: float32 [20], replicated, may hold values from 0.4 to 135
Outputs:
- block_out: bfloat16 [1, 16, 32, 72, 1280], P(None, 'view', 'row')
All inputs are finite; a program needn't handle non-finite values.
Results may differ from a plain program's by a relative error of at most 0.02.
Values may be sent and summed in bfloat16 or wider, within the bound.
No kernel may reach another device: no remote copies, remote signals or barrier semaphores. Data moves between devices by JAX's collectives and lax.ppermute only.
A program may use at most 192 MiB of HBM per device.

v0:
```python
import math

import jax
import jax.numpy as jnp
from jax import lax
from jax.sharding import PartitionSpec as P

GROUPS = 32


epsilon = 1e-05


def attend(query, key_block, value, head_scale):
    view_count = query.shape[0]
    item_count = query.shape[2]
    channels = query.shape[3]
    head_count = head_scale.shape[0]
    head_size = channels // head_count
    query_heads = query.reshape(view_count, item_count, head_count, head_size)
    key_heads = key_block.reshape(view_count, item_count, head_count, head_size)
    value_heads = value.reshape(view_count, item_count, head_count, head_size)
    scores = jnp.einsum(
        "vihd,uihd->ihvu", query_heads, key_heads, preferred_element_type=jnp.float32
    )
    scores = scores * (head_scale / math.sqrt(head_size))[None, :, None, None]
    peak_score = jnp.max(scores, axis=-1, keepdims=True)
    exp_scores = jnp.exp(scores - peak_score)
    soft_weights = (exp_scores / jnp.sum(exp_scores, axis=-1, keepdims=True)).astype(jnp.bfloat16)
    mixed = jnp.einsum(
        "ihvu,uihd->vihd", soft_weights, value_heads, preferred_element_type=jnp.float32
    )
    return mixed.astype(jnp.bfloat16).reshape(view_count, 1, item_count, channels)


def send_back(mixed):
    return lax.all_to_all(mixed, VIEW, split_axis=0, concat_axis=1, tiled=True)


def local(
    latent,
    gn_gain,
    gn_bias,
    cam_idx,
    noise_idx,
    cam_table,
    noise_table,
    conv_w,
    conv_bias,
    ln_gain,
    attn_in,
    attn_out,
    head_scale,
):
    samples, local_views, local_rows, local_cols, channels = latent.shape
    width_out = ln_gain.shape[0]
    out_part = conv_w.shape[-1]
    whole = lax.all_gather(latent, ROW, axis=2, tiled=True)
    whole, attn_in = lax.optimization_barrier((whole, attn_in))
    core = lax.axis_index("core")
    half_in = attn_in.shape[1] // 2
    half_out = attn_out.shape[1] // 2
    in_half = lax.dynamic_slice_in_dim(attn_in, core * half_in, half_in, axis=1)
    in_half = lax.all_gather(in_half, VIEW, axis=0, tiled=False)
    out_half = lax.dynamic_slice_in_dim(attn_out, core * half_out, half_out, axis=1)
    view_devices = lax.axis_size(VIEW)
    out_half = jnp.broadcast_to(out_half[None], (view_devices,) + out_half.shape)
    out_half = lax.all_to_all(out_half, VIEW, split_axis=0, concat_axis=0, tiled=True)
    out_half = out_half.reshape(-1, half_out)

    all_rows = whole.shape[2]
    x_float = whole.astype(jnp.float32)
    grouped = x_float.reshape(
        samples, local_views, all_rows, local_cols, GROUPS, channels // GROUPS
    )
    average = jnp.mean(grouped, axis=(2, 3, 5), keepdims=True)
    centred = grouped - average
    variance = jnp.mean(centred * centred, axis=(2, 3, 5), keepdims=True)
    normed = (centred * lax.rsqrt(variance + epsilon)).reshape(x_float.shape)
    cam_film = jnp.take(cam_table, cam_idx, axis=0).astype(jnp.float32)
    noise_film = jnp.take(noise_table, noise_idx, axis=0).astype(jnp.float32)
    film_rows = cam_film + noise_film[:, None, :]
    film_scale = film_rows[:, :, None, None, :channels]
    film_shift = film_rows[:, :, None, None, channels:]
    hidden = (normed * gn_gain + gn_bias) * (1.0 + film_scale) + film_shift
    activated = jax.nn.silu(hidden).astype(jnp.bfloat16)
    out_half, activated = lax.optimization_barrier((out_half, activated))
    taps = conv_w.shape[1]
    padded = jnp.pad(activated, ((0, 0), (0, 0), (1, 1), (0, 0), (0, 0)))
    tap_sum = None
    for tap_row in range(conv_w.shape[0]):
        rows_in = padded[:, :, tap_row : tap_row + all_rows].reshape(-1, channels)
        weight_row = jnp.transpose(conv_w[tap_row], (1, 0, 2)).reshape(channels, taps * out_part)
        part = jnp.dot(rows_in, weight_row, preferred_element_type=jnp.float32)
        tap_sum = part if tap_sum is None else tap_sum + part
    tap_sum = tap_sum.reshape(samples, local_views, all_rows, local_cols, taps, out_part)
    wide = jnp.pad(tap_sum, ((0, 0), (0, 0), (0, 0), (1, 1), (0, 0), (0, 0)))
    conv_out = (
        wide[:, :, :, 0:local_cols, 0]
        + wide[:, :, :, 1 : local_cols + 1, 1]
        + wide[:, :, :, 2 : local_cols + 2, 2]
    )
    me = lax.axis_index("chip") * lax.axis_size("core") + core
    bias_part = lax.dynamic_slice_in_dim(conv_bias, me * out_part, out_part)
    latent_part = lax.dynamic_slice_in_dim(whole, me * out_part, out_part, axis=4)
    resid_part = (latent_part.astype(jnp.float32) + conv_out + bias_part).astype(jnp.bfloat16)
    resid_out = lax.all_to_all(resid_part, ROW, split_axis=2, concat_axis=4, tiled=True)
    resid_float = resid_out.astype(jnp.float32)
    middle = jnp.mean(resid_float, axis=-1, keepdims=True)
    spread_y = jnp.mean((resid_float - middle) ** 2, axis=-1, keepdims=True)
    normed_y = ((resid_float - middle) * lax.rsqrt(spread_y + epsilon) * ln_gain).astype(
        jnp.bfloat16
    )
    view_devices = lax.axis_size(VIEW)
    per_device = samples * local_rows * local_cols // view_devices
    pixel_major = jnp.moveaxis(normed_y, 1, 0).reshape(
        local_views, view_devices, per_device, width_out
    )
    views = lax.all_to_all(pixel_major, VIEW, split_axis=1, concat_axis=0, tiled=True)
    in_half, views = lax.optimization_barrier((in_half, views))
    swap = [(0, 1), (1, 0)]
    in_other = lax.ppermute(in_half, "core", swap)
    flat_block = views.reshape(-1, width_out)
    block_mine = lax.dynamic_slice_in_dim(flat_block, core * half_in, half_in, axis=1)
    block_other = lax.dynamic_slice_in_dim(flat_block, (1 - core) * half_in, half_in, axis=1)
    triple_in = jnp.einsum(
        "pc,jmcd->mpjd", block_mine, in_half, preferred_element_type=jnp.float32
    ) + jnp.einsum(
        "pc,jmcd->mpjd", block_other, in_other, preferred_element_type=jnp.float32
    )
    triple_in = triple_in.astype(jnp.bfloat16).reshape((3,) + views.shape)
    mixed = send_back(attend(triple_in[0], triple_in[1], triple_in[2], head_scale))
    out_half, mixed = lax.optimization_barrier((out_half, mixed))
    out_other = lax.ppermute(out_half, "core", swap)
    mixed = jnp.moveaxis(
        mixed.reshape(local_views, samples, local_rows, local_cols, width_out), 0, 1
    )
    flat_mixed = mixed.reshape(-1, width_out)
    cols_mine = jnp.dot(flat_mixed, out_half, preferred_element_type=jnp.float32)
    cols_other = jnp.dot(flat_mixed, out_other, preferred_element_type=jnp.float32)
    projected = jnp.where(
        core == 0,
        jnp.concatenate([cols_mine, cols_other], axis=1),
        jnp.concatenate([cols_other, cols_mine], axis=1),
    )
    return (resid_float + projected.reshape(resid_float.shape)).astype(jnp.bfloat16)

ROW = ("chip", "core")
VIEW = ("vz", "vy")


def solution(mesh):
    cores = 2
    split = jax.sharding.Mesh(
        mesh.devices.reshape(
            mesh.shape["view"] // 2, 2, mesh.shape["row"] // cores, cores
        ),
        ("vz", "vy", "chip", "core"),
    )
    placed = (
        P(None, VIEW, ROW, None, None),
        P(),
        P(),
        P(None, VIEW),
        P(),
        P(),
        P(),
        P(None, None, None, ROW),
        P(),
        P(),
        P(None, None, VIEW),
        P(VIEW, None),
        P(),
    )
    return jax.shard_map(
        local,
        mesh=split,
        in_specs=placed,
        out_specs=P(None, VIEW, ROW, None, None),
        check_vma=False,
    )
```

profile of v0, /device:TPU:1, one launch (start us, length us, event | category | flops | bytes accessed | tf_op | source)
XLA Modules:
  0.0 265.4 jit_solution(4191928589715170726)
XLA Ops:
  9.5 11.7 %all-to-all-start = ((bf16[16,80,640]{2,1,0:T(8,128)(2,1)}), bf16[16,80,640]{2,1,0:T(8,128)(2,1)S(1)}, u32[]{:S(2)}, u32[]{:S(2)}) async-start(bf16[16,80,640]{2,1,0:T(8,128)(2,1)} %broadcast_in_dim.26), calls=%async_computation | async-start | bytes 3276800 | tf_op jit(solution)/shard_map/all_to_all | solution.py:68
  24.3 2.9 %fusion.54 = (bf16[1,3,1280,80]{2,3,1,0:T(8,128)(2,1)S(1)}, bf16[1,3,1280,80]{2,3,1,0:T(8,128)(2,1)}, bf16[1,3,1280,80]{2,3,1,0:T(8,128)(2,1)}) fusion(bf16[3,3,1280,80]{2,3,1,0:T(8,128)(2,1)} %param.20), kind=kLoop, calls=%fused_computation.75 | loop fusion | bytes 3686400 | tf_op jit(solution)/shard_map/slice | solution.py:93
  27.1 44.7 %all-gather.4.cloned.1.call-done = bf16[1,1,32,72,1280]{4,3,1,0,2:T(8,128)(2,1)} async-done(((bf16[1,1,2,72,1280]{4,3,1,0,2:T(8,128)(2,1)}), bf16[1,1,32,72,1280]{4,3,1,0,2:T(8,128)(2,1)}) %all-gather.4.cloned.1.call-update) | async-done | bytes 5898256 | tf_op jit(solution)/shard_map/all_gather | solution.py:58
  72.6 3.5 %convert_reduce_fusion = f32[1280]{0:T(1024)S(1)} fusion(bf16[1,1,32,72,1280]{4,3,1,0,2:T(8,128)(2,1)} %all-gather.4.cloned.1.call-done), kind=kLoop, calls=%fused_computation.2 | loop fusion | flops 5896960 | bytes 5903360 | tf_op jit(solution)/shard_map/reduce_sum | solution.py:76
  76.2 15.0 %copy.96 = bf16[1,1,32,72,1280]{3,2,4,1,0:T(8,128)(2,1)} copy(bf16[1,1,32,72,1280]{4,3,1,0,2:T(8,128)(2,1)} %all-gather.4.cloned.1.call-done) | data formatting | bytes 11796480 | tf_op jit(solution)/shard_map/optimization_barrier | solution.py:59
  91.6 4.3 %fusion.3 = f32[1280]{0:T(1024)S(1)} fusion(bf16[1,1,32,72,1280]{4,3,1,0,2:T(8,128)(2,1)} %all-gather.4.cloned.1.call-done, f32[1280]{0:T(1024)S(1)} %sub.57), kind=kLoop, calls=%fused_computation.5 | loop fusion | flops 11795200 | bytes 5908480 | tf_op jit(solution)/shard_map/reduce_sum | solution.py:78
  96.3 8.3 %multiply_convert_fusion = bf16[1,1,32,72,1280]{4,3,2,1,0:T(8,128)(2,1)} fusion(bf16[1,1,32,72,1280]{4,3,1,0,2:T(8,128)(2,1)} %all-gather.4.cloned.1.call-done, f32[1280]{0:T(1024)S(1)} %get-tuple-element.44, f32[1280]{0:T(1024)S(1)} %get-tuple-element.43, f32[1280]{0:T(1024)S(1)} %copy-done.8, f32[1280]{0:T(1024)S(1)} %copy-done.9, f32[1280]{0:T(1024)S(1)} %mul.110, ...), kind=kLoop, calls=%fused_computation.10 | loop fusion | flops 35389440 | bytes 11827200 | tf_op jit(solution)/shard_map/convert_element_type | solution.py:86
  104.6 5.6 %pad_slice_fusion = (bf16[1,1,32,72,1280]{4,3,2,1,0:T(8,128)(2,1)S(1)}, bf16[1,1,32,72,1280]{4,3,2,1,0:T(8,128)(2,1)S(1)}) fusion(bf16[1,1,32,72,1280]{4,3,2,1,0:T(8,128)(2,1)} %multiply_convert_fusion), kind=kLoop, calls=%fused_computation.11 | loop fusion | bytes 17694720 | tf_op jit(solution)/shard_map/slice | solution.py:92
  110.3 1.7 fusion.61
  113.1 1.8 convolution_add_fusion.1
  114.9 1.8 convolution_add_fusion
  116.7 5.3 %reshape.380 = f32[1,1,32,72,3,80]{3,2,5,4,1,0:T(8,128)} reshape(f32[2304,240]{0,1:T(8,128)S(1)} %convolution_add_fusion) | data formatting | bytes 4423680 | tf_op jit(solution)/shard_map/reshape | solution.py:96
  121.9 3.1 %fusion.20 = bf16[1,1,32,72,80]{3,2,4,1,0:T(8,128)(2,1)S(1)} fusion(f32[1,1,32,72,3,80]{3,2,5,4,1,0:T(8,128)} %reshape.380, f32[80]{0:T(128)S(1)} %dynamic_slice.20, bf16[1,1,32,72,1280]{3,2,4,1,0:T(8,128)(2,1)} %copy.96, s32[]{:T(128)S(6)} %select_n.65), kind=kLoop, calls=%fused_computation.33 | loop fusion | flops 1105920 | bytes 6267204 | tf_op jit(solution)/shard_map/convert_element_type | solution.py:106
  125.8 15.3 %all_to_all.38 = bf16[1,1,32,72,80]{4,3,1,0,2:T(8,128)(2,1)S(1)} all-to-all(bf16[1,1,32,72,80]{4,3,1,0,2:T(8,128)(2,1)S(1)} %copy.98), channel_id=1, replica_groups=mesh['vz'=8,'vy'=2,'chip'=8,'core'=2] {'chip','core'}, dimensions={2} | all-to-all | bytes 737280 | tf_op jit(solution)/shard_map/all_to_all | solution.py:107
  142.1 2.0 multiply_reduce_fusion
  144.3 1.4 reshape.432
  146.1 33.9 %all_to_all.39 = bf16[1,16,9,1280]{3,2,0,1:T(8,128)(2,1)S(1)} all-to-all(bf16[1,16,9,1280]{3,2,0,1:T(8,128)(2,1)S(1)} %copy.103), channel_id=1, replica_groups=mesh['vz'=8,'vy'=2,'chip'=8,'core'=2] {'vz','vy'}, dimensions={1} | all-to-all | bytes 737280 | tf_op jit(solution)/shard_map/all_to_all | solution.py:119
  180.1 11.9 %all-gather.6.cloned.1.call-done = bf16[48,640,80]{1,2,0:T(8,128)(2,1)} async-done(((bf16[3,640,80]{1,2,0:T(8,128)(2,1)}), bf16[48,640,80]{1,2,0:T(8,128)(2,1)}) %all-gather.6.cloned.1.call-update) | async-done | bytes 4915216 | tf_op jit(solution)/shard_map/all_gather | solution.py:64
  192.1 1.7 collective-permute-start
  194.0 5.1 %fusion.38 = f32[16,3,80,144]{2,3,1,0:T(8,128)S(1)} fusion(bf16[16,3,640,80]{2,3,1,0:T(8,128)(2,1)} %bitcast.111, bf16[144,1280]{1,0:T(8,128)(2,1)S(1)} %reshape.381, s32[]{:T(128)S(6)} %select_n.66), kind=kOutput, calls=%fused_computation.52 | convolution fusion | flops 707788800 | bytes 7311364 | tf_op jit(solution)/shard_map/pc,jmcd->mpjd/dot_general | solution.py:126
  199.1 2.7 %collective-permute-done = bf16[16,3,640,80]{2,3,1,0:T(8,128)(2,1)} collective-permute-done((bf16[16,3,640,80]{2,3,1,0:T(8,128)(2,1)}, bf16[16,3,640,80]{2,3,1,0:T(8,128)(2,1)}, u32[]{:S(2)}, u32[]{:S(2)}) %collective-permute-start) | collective-permute-done | bytes 4915232 | tf_op jit(solution)/shard_map/ppermute | solution.py:122
  201.9 5.1 %fusion.13 = bf16[3,144,16,80]{3,1,0,2:T(8,128)(2,1)S(1)} fusion(f32[16,3,80,144]{2,3,1,0:T(8,128)S(1)} %fusion.38, bf16[16,3,640,80]{2,3,1,0:T(8,128)(2,1)} %collective-permute-done, bf16[144,1280]{1,0:T(8,128)(2,1)S(1)} %reshape.381, s32[]{:T(128)S(6)} %select_n.72), kind=kOutput, calls=%fused_computation.23 | convolution fusion | flops 708894720 | bytes 9744388 | tf_op jit(solution)/shard_map/pc,jmcd->mpjd/dot_general | solution.py:128
  208.1 3.1 %reshape_squeeze.10 = bf16[16,9,20,64]{3,2,1,0:T(8,128)(2,1)} reshape(bf16[1,144,16,80]{3,2,1,0:T(8,128)(2,1)} %copy.107) | data formatting | bytes 737280 | tf_op jit(solution)/shard_map/reshape;squeeze | solution.py:20
  211.4 2.2 reshape_squeeze.11
  213.7 2.2 reshape_squeeze.9
  215.9 3.5 %fusion.56 = (f32[9,20,16]{2,1,0:T(8,128)S(1)}, f32[9,20,16,16]{2,3,1,0:T(8,128)}) fusion(bf16[16,9,20,64]{3,2,1,0:T(8,128)(2,1)} %reshape_squeeze.11, bf16[16,9,20,64]{3,2,1,0:T(8,128)(2,1)} %reshape_squeeze.10, f32[20]{0:T(128)S(1)} %broadcast_multiply_fusion.1), kind=kOutput, calls=%fused_computation.77 | convolution fusion | flops 6036495 | bytes 933200 | tf_op jit(solution)/shard_map/sub | solution.py:28
  219.4 1.8 fusion.21
  221.5 1.5 reshape.452
  222.9 27.0 %all_to_all.40 = bf16[16,1,9,1280]{3,2,1,0:T(8,128)(2,1)} all-to-all(bf16[16,1,9,1280]{3,2,1,0:T(8,128)(2,1)} %reshape.452), channel_id=1, replica_groups=mesh['vz'=8,'vy'=2,'chip'=8,'core'=2] {'vz','vy'}, dimensions={0} | all-to-all | bytes 737280 | tf_op jit(solution)/shard_map/all_to_all | solution.py:37
  250.0 2.0 collective-permute-start.1
  253.8 1.9 fusion.22
  255.7 1.9 fusion.25
  (68 shorter events, 14.2 us)
Async XLA Ops:
  6.5 65.3 %copy-start = (bf16[3,1280,80]{1,2,0:T(8,128)(2,1)S(1)}, bf16[3,1280,80]{1,2,0:T(8,128)(2,1)}, u32[]{:S(2)}) copy-start(bf16[3,1280,80]{1,2,0:T(8,128)(2,1)} %param.23) | copy-start | bytes 1843204
  6.5 65.3 %all-gather.4.cloned.1.call-start = ((), (), s32[]{:S(2)}) async-start(), calls=%async_computation.4 | async-start | bytes 6266880 | tf_op jit(solution)/shard_map/all_gather | solution.py:58
  9.5 95.1 %all-to-all-start = ((bf16[16,80,640]{2,1,0:T(8,128)(2,1)}), bf16[16,80,640]{2,1,0:T(8,128)(2,1)S(1)}, u32[]{:S(2)}, u32[]{:S(2)}) async-start(bf16[16,80,640]{2,1,0:T(8,128)(2,1)} %broadcast_in_dim.26), calls=%async_computation | async-start | bytes 3276800 | tf_op jit(solution)/shard_map/all_to_all | solution.py:68
  21.2 170.8 %all-gather.6.cloned.1.call-start = ((), (), s32[]{:S(2)}) async-start(), calls=%async_computation.5 | async-start | bytes 5222400 | tf_op jit(solution)/shard_map/all_gather | solution.py:64
  91.2 5.0 %copy-start.8 = (f32[1280]{0:T(1024)S(1)}, f32[1280]{0:T(1024)}, u32[]{:S(2)}) copy-start(f32[1280]{0:T(1024)} %param.15) | copy-start | bytes 15364
  91.2 5.1 %copy-start.9 = (f32[1280]{0:T(1024)S(1)}, f32[1280]{0:T(1024)}, u32[]{:S(2)}) copy-start(f32[1280]{0:T(1024)} %param.14) | copy-start | bytes 15364
  104.6 5.7 %copy-start.3 = (bf16[16,80,640]{2,1,0:T(8,128)(2,1)}, bf16[16,80,640]{2,1,0:T(8,128)(2,1)S(1)}, u32[]{:S(2)}) copy-start(bf16[16,80,640]{2,1,0:T(8,128)(2,1)S(1)} %all-to-all-done) | copy-start | bytes 4915204
  104.6 5.7 %copy-start.6 = (bf16[1,3,1280,80]{2,3,1,0:T(8,128)(2,1)S(1)}, bf16[1,3,1280,80]{2,3,1,0:T(8,128)(2,1)}, u32[]{:S(2)}) copy-start(bf16[1,3,1280,80]{2,3,1,0:T(8,128)(2,1)} %get-tuple-element.48) | copy-start | bytes 1843204
  110.3 2.7 %copy-start.2 = (bf16[1,1,32,72,1280]{4,3,2,1,0:T(8,128)(2,1)S(1)}, bf16[1,1,32,72,1280]{4,3,2,1,0:T(8,128)(2,1)}, u32[]{:S(2)}) copy-start(bf16[1,1,32,72,1280]{4,3,2,1,0:T(8,128)(2,1)} %multiply_convert_fusion) | copy-start | bytes 17694724
  110.3 2.8 %copy-start.4 = (bf16[1,3,1280,80]{2,3,1,0:T(8,128)(2,1)S(1)}, bf16[1,3,1280,80]{2,3,1,0:T(8,128)(2,1)}, u32[]{:S(2)}) copy-start(bf16[1,3,1280,80]{2,3,1,0:T(8,128)(2,1)} %get-tuple-element.49) | copy-start | bytes 1843204
  141.1 4.6 %copy-start.7 = (f32[1280]{0:T(1024)S(1)}, f32[1280]{0:T(1024)}, u32[]{:S(2)}) copy-start(f32[1280]{0:T(1024)} %param.22) | copy-start | bytes 15364
  142.0 51.7 %copy-start.10 = (f32[20]{0:T(128)S(1)}, f32[20]{0:T(128)}, u32[]{:S(2)}) copy-start(f32[20]{0:T(128)} %param.25) | copy-start | bytes 244
  192.1 9.8 %collective-permute-start = (bf16[16,3,640,80]{2,3,1,0:T(8,128)(2,1)}, bf16[16,3,640,80]{2,3,1,0:T(8,128)(2,1)}, u32[]{:S(2)}, u32[]{:S(2)}) collective-permute-start(bf16[16,3,640,80]{2,3,1,0:T(8,128)(2,1)} %bitcast.110), channel_id=1, source_target_pairs={{0,1},{1,0},{2,3},{3,2},{4,5},{5,4},{6,7},{7,6},{8,9},{9,8},{10,11... | collective-permute-start | bytes 14745608 | tf_op jit(solution)/shard_map/ppermute | solution.py:122
  215.9 3.5 %copy-start.5 = (bf16[16,9,20,64]{3,2,1,0:T(8,128)(2,1)S(1)}, bf16[16,9,20,64]{3,2,1,0:T(8,128)(2,1)}, u32[]{:S(2)}) copy-start(bf16[16,9,20,64]{3,2,1,0:T(8,128)(2,1)} %reshape_squeeze.9) | copy-start | bytes 1105924
  250.0 5.7 %collective-permute-start.1 = (bf16[1280,640]{1,0:T(8,128)(2,1)}, bf16[1280,640]{1,0:T(8,128)(2,1)}, u32[]{:S(2)}, u32[]{:S(2)}) collective-permute-start(bf16[1280,640]{1,0:T(8,128)(2,1)} %bitcast.114), channel_id=1, source_target_pairs={{0,1},{1,0},{2,3},{3,2},{4,5},{5,4},{6,7},{7,6},{8,9},{9,8},{10,11... | collective-permute-start | bytes 4915208 | tf_op jit(solution)/shard_map/ppermute | solution.py:134
  252.0 6.5 %copy-start.1 = (bf16[3,1280,80]{1,2,0:T(8,128)(2,1)S(1)}, bf16[3,1280,80]{1,2,0:T(8,128)(2,1)}, u32[]{:S(2)}) copy-start(bf16[3,1280,80]{1,2,0:T(8,128)(2,1)} %param.23) | copy-start | bytes 1843204
Sparse Core Ops, SparseCore 0:
  9.2 62.6 all-gather.3
  74.5 117.5 all-gather.5
where the time goes:
time: 267 us; the launch traced here: 265 us
  blocking collectives  76.3 us (29%)
  waiting for transfers between devices  60.1 us (23%)
  local copies, waits for them, and re-layouts  49.6 us (19%)
  matrix products  24.7 us (9%)
  other arithmetic  24.2 us (9%)
  starting transfers between devices  15.5 us (6%)
  between operations  15 us (6%)
    all_gather x1, waiting for transfers between devices, local(): whole = lax.all_gather(latent, ROW, axis=2, tiled=True)  44.7 us
    all_to_all x1, blocking collectives, local(): lax.all_to_all(pixel_major, VIEW, split_axis=1, concat_axis=0, tiled=True)  33.9 us
    all_to_all x1, blocking collectives, send_back(): return lax.all_to_all(mixed, VIEW, split_axis=0, concat_axis=1, tiled=True)  27 us
    all_to_all x1, blocking collectives, local(): lax.all_to_all(resid_part, ROW, split_axis=2, concat_axis=4, tiled=True)  15.3 us
    optimization_barrier x1, local copies, waits for them, and re-layouts, local(): whole, attn_in = lax.optimization_barrier((whole, attn_in))  15 us
    all_gather x1, waiting for transfers between devices, local(): in_half = lax.all_gather(in_half, VIEW, axis=0, tiled=False)  11.9 us
    all_to_all x1, starting transfers between devices, local(): lax.all_to_all(out_half, VIEW, split_axis=0, concat_axis=0, tiled=True)  11.7 us
    convert_element_type x1, other arithmetic, local(): activated = jax.nn.silu(hidden).astype(jnp.bfloat16)  8.33 us
  transfers between devices with their start and end apart: 5, of which 3 were waited for; matrix products, arithmetic and copies ran while one was open for 28% of the time, Pallas kernels for 0%

commit v1 on v0

--- a/solution.py
+++ b/solution.py
@@ -101,10 +101,11 @@
         + wide[:, :, :, 2 : local_cols + 2, 2]
     )
     me = lax.axis_index("chip") * lax.axis_size("core") + core
-    bias_part = lax.dynamic_slice_in_dim(conv_bias, me * out_part, out_part)
-    latent_part = lax.dynamic_slice_in_dim(whole, me * out_part, out_part, axis=4)
-    resid_part = (latent_part.astype(jnp.float32) + conv_out + bias_part).astype(jnp.bfloat16)
-    resid_out = lax.all_to_all(resid_part, ROW, split_axis=2, concat_axis=4, tiled=True)
+    conv_part = conv_out.astype(jnp.bfloat16)
+    conv_rows = lax.all_to_all(conv_part, ROW, split_axis=2, concat_axis=4, tiled=True)
+    resid_out = (
+        latent.astype(jnp.float32) + conv_rows.astype(jnp.float32) + conv_bias
+    ).astype(jnp.bfloat16)
     resid_float = resid_out.astype(jnp.float32)
     middle = jnp.mean(resid_float, axis=-1, keepdims=True)
     spread_y = jnp.mean((resid_float - middle) ** 2, axis=-1, keepdims=True)

time: 267 us -> 257 us (0.963)
  local copies, waits for them, and re-layouts: 49.6 us -> 29.9 us
  waiting for transfers between devices: 60.1 us -> 76.4 us
  blocking collectives: 76.3 us -> 72.1 us
    optimization_barrier x2 -> x0, local copies, waits for them, and re-layouts: 15.2 us -> none  [the longest x1 15 us: local(): whole, attn_in = lax.optimization_barrier((whole, attn_in))]
    all_gather x1, waiting for transfers between devices: 11.9 us -> 25.6 us  [local(): in_half = lax.all_gather(in_half, VIEW, axis=0, tiled=False)]
    all_to_all x1, blocking collectives: 33.9 us -> 31.2 us  [local(): lax.all_to_all(pixel_major, VIEW, split_axis=1, concat_axis=0, tiled=True)]
  transfers between devices with their start and end apart: 5 -> 5, of which waited for: 3 -> 4; matrix products, arithmetic and copies ran while one was open for 28% -> 20% of each run, Pallas kernels for 0% -> 0%
where the time goes in v1:
time: 257 us; the launch traced here: 256 us
  waiting for transfers between devices  76.4 us (30%)
  blocking collectives  72.1 us (28%)
  local copies, waits for them, and re-layouts  29.9 us (12%)
  matrix products  23.2 us (9%)
  other arithmetic  22 us (9%)
  starting transfers between devices  17.1 us (7%)
  between operations  15 us (6%)
    all_gather x1, waiting for transfers between devices, local(): whole = lax.all_gather(latent, ROW, axis=2, tiled=True)  45.7 us
    all_to_all x1, blocking collectives, local(): lax.all_to_all(pixel_major, VIEW, split_axis=1, concat_axis=0, tiled=True)  31.2 us
    all_to_all x1, blocking collectives, send_back(): return lax.all_to_all(mixed, VIEW, split_axis=0, concat_axis=1, tiled=True)  25.7 us
    all_gather x1, waiting for transfers between devices, local(): in_half = lax.all_gather(in_half, VIEW, axis=0, tiled=False)  25.6 us
    all_to_all x1, blocking collectives, local(): lax.all_to_all(conv_part, ROW, split_axis=2, concat_axis=4, tiled=True)  15.3 us
    all_to_all x1, starting transfers between devices, local(): lax.all_to_all(out_half, VIEW, split_axis=0, concat_axis=0, tiled=True)  11.7 us
    convert_element_type x1, other arithmetic, local(): activated = jax.nn.silu(hidden).astype(jnp.bfloat16)  8.54 us
    slice x1, local copies, waits for them, and re-layouts, local(): rows_in = padded[:, :, tap_row:tap_row + all_rows].reshape(-1, channels)  5.63 us
  transfers between devices with their start and end apart: 5, of which 4 were waited for; matrix products, arithmetic and copies ran while one was open for 20% of the time, Pallas kernels for 0%

profile of v1, /device:TPU:1, one launch (start us, length us, event | category | flops | bytes accessed | tf_op | source)
XLA Modules:
  0.0 255.8 jit_solution(13548675911080410009)
XLA Ops:
  8.2 1.3 broadcast_in_dim.26
  9.5 11.7 %all-to-all-start = ((bf16[16,80,640]{2,1,0:T(8,128)(2,1)}), bf16[16,80,640]{2,1,0:T(8,128)(2,1)S(1)}, u32[]{:S(2)}, u32[]{:S(2)}) async-start(bf16[16,80,640]{2,1,0:T(8,128)(2,1)} %broadcast_in_dim.26), calls=%async_computation | async-start | bytes 3276800 | tf_op jit(solution)/shard_map/all_to_all | solution.py:68
  23.5 2.6 %fusion.52 = (bf16[1,3,1280,80]{2,3,1,0:T(8,128)(2,1)S(1)}, bf16[1,3,1280,80]{2,3,1,0:T(8,128)(2,1)}, bf16[1,3,1280,80]{2,3,1,0:T(8,128)(2,1)}) fusion(bf16[3,3,1280,80]{2,3,1,0:T(8,128)(2,1)} %param.20), kind=kLoop, calls=%fused_computation.74 | loop fusion | bytes 3686400 | tf_op jit(solution)/shard_map/slice | solution.py:93
  26.1 45.7 %all-gather.4.cloned.1.call-done = bf16[1,1,32,72,1280]{4,3,1,0,2:T(8,128)(2,1)} async-done(((bf16[1,1,2,72,1280]{4,3,1,0,2:T(8,128)(2,1)}), bf16[1,1,32,72,1280]{4,3,1,0,2:T(8,128)(2,1)}) %all-gather.4.cloned.1.call-update) | async-done | bytes 5898256 | tf_op jit(solution)/shard_map/all_gather | solution.py:58
  72.7 3.5 %convert_reduce_fusion = f32[1280]{0:T(1024)S(1)} fusion(bf16[1,1,32,72,1280]{4,3,1,0,2:T(8,128)(2,1)} %all-gather.4.cloned.1.call-done), kind=kLoop, calls=%fused_computation.2 | loop fusion | flops 5896960 | bytes 5903360 | tf_op jit(solution)/shard_map/reduce_sum | solution.py:76
  76.6 4.3 %fusion.3 = f32[1280]{0:T(1024)S(1)} fusion(bf16[1,1,32,72,1280]{4,3,1,0,2:T(8,128)(2,1)} %all-gather.4.cloned.1.call-done, f32[1280]{0:T(1024)S(1)} %sub.42), kind=kLoop, calls=%fused_computation.5 | loop fusion | flops 11795200 | bytes 5908480 | tf_op jit(solution)/shard_map/reduce_sum | solution.py:78
  81.2 8.5 %multiply_convert_fusion = bf16[1,1,32,72,1280]{4,3,1,0,2:T(8,128)(2,1)} fusion(bf16[1,1,32,72,1280]{4,3,1,0,2:T(8,128)(2,1)} %all-gather.4.cloned.1.call-done, f32[1280]{0:T(1024)S(1)} %get-tuple-element.44, f32[1280]{0:T(1024)S(1)} %get-tuple-element.43, f32[1280]{0:T(1024)S(1)} %copy-done.11, f32[1280]{0:T(1024)S(1)} %copy-done.12, f32[1280]{0:T(1024)S(1)} %mul.83, ...), kind=kLoop, calls=%fused_computation.10 | loop fusion | flops 35389440 | bytes 11827200 | tf_op jit(solution)/shard_map/convert_element_type | solution.py:86
  89.8 5.6 %pad_slice_fusion = (bf16[1,1,32,72,1280]{4,3,1,0,2:T(8,128)(2,1)S(1)}, bf16[1,1,32,72,1280]{4,3,1,0,2:T(8,128)(2,1)S(1)}) fusion(bf16[1,1,32,72,1280]{4,3,1,0,2:T(8,128)(2,1)} %multiply_convert_fusion), kind=kLoop, calls=%fused_computation.11 | loop fusion | bytes 17694720 | tf_op jit(solution)/shard_map/slice | solution.py:92
  95.5 1.7 fusion.59
  97.2 0.9 copy-done.2
  98.3 1.8 convolution_add_fusion.1
  100.1 1.8 convolution_add_fusion
  101.8 5.2 %reshape.319 = f32[1,1,32,72,3,80]{3,2,5,4,1,0:T(8,128)} reshape(f32[2304,240]{0,1:T(8,128)S(1)} %convolution_add_fusion) | data formatting | bytes 4423680 | tf_op jit(solution)/shard_map/reshape | solution.py:96
  107.1 2.9 %fusion.35 = bf16[1,1,32,72,80]{3,2,4,1,0:T(8,128)(2,1)S(1)} fusion(f32[1,1,32,72,3,80]{3,2,5,4,1,0:T(8,128)} %reshape.319), kind=kLoop, calls=%fused_computation.50 | loop fusion | flops 552960 | bytes 5611520 | tf_op jit(solution)/shard_map/convert_element_type | solution.py:104
  110.8 15.3 %all_to_all.38 = bf16[1,1,32,72,80]{4,3,1,0,2:T(8,128)(2,1)S(1)} all-to-all(bf16[1,1,32,72,80]{4,3,1,0,2:T(8,128)(2,1)S(1)} %copy.40), channel_id=1, replica_groups=mesh['vz'=8,'vy'=2,'chip'=8,'core'=2] {'chip','core'}, dimensions={2} | all-to-all | bytes 737280 | tf_op jit(solution)/shard_map/all_to_all | solution.py:105
  127.7 31.2 %all_to_all.39 = bf16[1,16,9,1280]{3,2,0,1:T(8,128)(2,1)S(1)} all-to-all(bf16[1,16,9,1280]{3,2,0,1:T(8,128)(2,1)S(1)} %bitcast.99), channel_id=1, replica_groups=mesh['vz'=8,'vy'=2,'chip'=8,'core'=2] {'vz','vy'}, dimensions={1} | all-to-all | bytes 737280 | tf_op jit(solution)/shard_map/all_to_all | solution.py:120
  158.8 25.6 %all-gather.6.cloned.1.call-done = bf16[48,640,80]{1,2,0:T(8,128)(2,1)} async-done(((bf16[3,640,80]{1,2,0:T(8,128)(2,1)}), bf16[48,640,80]{1,2,0:T(8,128)(2,1)}) %all-gather.6.cloned.1.call-update) | async-done | bytes 4915216 | tf_op jit(solution)/shard_map/all_gather | solution.py:64
  184.4 3.3 %collective-permute-start = (bf16[16,3,640,80]{2,3,1,0:T(8,128)(2,1)}, bf16[16,3,640,80]{2,3,1,0:T(8,128)(2,1)}, u32[]{:S(2)}, u32[]{:S(2)}) collective-permute-start(bf16[16,3,640,80]{2,3,1,0:T(8,128)(2,1)} %bitcast.91), channel_id=1, source_target_pairs={{0,1},{1,0},{2,3},{3,2},{4,5},{5,4},{6,7},{7,6},{8,9},{9,8},{10,11... | collective-permute-start | bytes 14745608 | tf_op jit(solution)/shard_map/ppermute | solution.py:123
  187.9 5.1 %fusion.37 = f32[16,3,80,144]{2,3,1,0:T(8,128)S(1)} fusion(bf16[16,3,640,80]{2,3,1,0:T(8,128)(2,1)} %bitcast.92, bf16[144,1280]{1,0:T(8,128)(2,1)S(1)} %reshape.320, s32[]{:T(128)S(6)} %select_n.60), kind=kOutput, calls=%fused_computation.52 | convolution fusion | flops 707788800 | bytes 7311364 | tf_op jit(solution)/shard_map/pc,jmcd->mpjd/dot_general | solution.py:127
  192.9 2.9 %collective-permute-done = bf16[16,3,640,80]{2,3,1,0:T(8,128)(2,1)} collective-permute-done((bf16[16,3,640,80]{2,3,1,0:T(8,128)(2,1)}, bf16[16,3,640,80]{2,3,1,0:T(8,128)(2,1)}, u32[]{:S(2)}, u32[]{:S(2)}) %collective-permute-start) | collective-permute-done | bytes 4915232 | tf_op jit(solution)/shard_map/ppermute | solution.py:123
  195.8 5.1 %fusion.13 = bf16[3,144,16,80]{3,1,0,2:T(8,128)(2,1)S(1)} fusion(f32[16,3,80,144]{2,3,1,0:T(8,128)S(1)} %fusion.37, bf16[16,3,640,80]{2,3,1,0:T(8,128)(2,1)} %collective-permute-done, bf16[144,1280]{1,0:T(8,128)(2,1)S(1)} %reshape.320, s32[]{:T(128)S(6)} %select_n.66), kind=kOutput, calls=%fused_computation.23 | convolution fusion | flops 708894720 | bytes 9744388 | tf_op jit(solution)/shard_map/pc,jmcd->mpjd/dot_general | solution.py:129
  201.2 2.2 reshape_squeeze.10
  203.6 2.2 reshape_squeeze.11
  205.9 2.2 reshape_squeeze.9
  208.2 3.2 %fusion.54 = (f32[9,20,16]{2,1,0:T(8,128)S(1)}, f32[9,20,16,16]{2,3,1,0:T(8,128)}) fusion(bf16[16,9,20,64]{3,2,1,0:T(8,128)(2,1)} %reshape_squeeze.11, bf16[16,9,20,64]{3,2,1,0:T(8,128)(2,1)S(1)} %copy-done.7, f32[20]{0:T(128)S(1)} %broadcast_multiply_fusion.1), kind=kOutput, calls=%fused_computation.76 | convolution fusion | flops 6036495 | bytes 933200 | tf_op jit(solution)/shard_map/sub | solution.py:28
  211.3 2.2 fusion.18
  213.8 1.5 reshape.388
  215.2 25.7 %all_to_all.40 = bf16[16,1,9,1280]{3,2,1,0:T(8,128)(2,1)} all-to-all(bf16[16,1,9,1280]{3,2,1,0:T(8,128)(2,1)} %reshape.388), channel_id=1, replica_groups=mesh['vz'=8,'vy'=2,'chip'=8,'core'=2] {'vz','vy'}, dimensions={0} | all-to-all | bytes 737280 | tf_op jit(solution)/shard_map/all_to_all | solution.py:37
  240.9 2.0 collective-permute-start.1
  242.9 1.3 reshape.322
  244.7 1.5 collective-permute-done.1
  246.2 1.9 fusion.22
  (64 shorter events, 8.8 us)
Async XLA Ops:
  6.5 65.3 %copy-start = (bf16[3,1280,80]{1,2,0:T(8,128)(2,1)S(1)}, bf16[3,1280,80]{1,2,0:T(8,128)(2,1)}, u32[]{:S(2)}) copy-start(bf16[3,1280,80]{1,2,0:T(8,128)(2,1)} %param.23) | copy-start | bytes 1843204
  6.5 65.3 %all-gather.4.cloned.1.call-start = ((), (), s32[]{:S(2)}) async-start(), calls=%async_computation.4 | async-start | bytes 6266880 | tf_op jit(solution)/shard_map/all_gather | solution.py:58
  9.5 80.3 %all-to-all-start = ((bf16[16,80,640]{2,1,0:T(8,128)(2,1)}), bf16[16,80,640]{2,1,0:T(8,128)(2,1)S(1)}, u32[]{:S(2)}, u32[]{:S(2)}) async-start(bf16[16,80,640]{2,1,0:T(8,128)(2,1)} %broadcast_in_dim.26), calls=%async_computation | async-start | bytes 3276800 | tf_op jit(solution)/shard_map/all_to_all | solution.py:68
  21.3 163.1 %all-gather.6.cloned.1.call-start = ((), (), s32[]{:S(2)}) async-start(), calls=%async_computation.5 | async-start | bytes 5222400 | tf_op jit(solution)/shard_map/all_gather | solution.py:64
  72.6 8.6 %copy-start.11 = (f32[1280]{0:T(1024)S(1)}, f32[1280]{0:T(1024)}, u32[]{:S(2)}) copy-start(f32[1280]{0:T(1024)} %param.15) | copy-start | bytes 15364
  72.6 8.6 %copy-start.12 = (f32[1280]{0:T(1024)S(1)}, f32[1280]{0:T(1024)}, u32[]{:S(2)}) copy-start(f32[1280]{0:T(1024)} %param.14) | copy-start | bytes 15364
  89.8 5.6 %copy-start.3 = (bf16[16,80,640]{2,1,0:T(8,128)(2,1)}, bf16[16,80,640]{2,1,0:T(8,128)(2,1)S(1)}, u32[]{:S(2)}) copy-start(bf16[16,80,640]{2,1,0:T(8,128)(2,1)S(1)} %all-to-all-done) | copy-start | bytes 4915204
  89.8 5.7 %copy-start.8 = (bf16[1,3,1280,80]{2,3,1,0:T(8,128)(2,1)S(1)}, bf16[1,3,1280,80]{2,3,1,0:T(8,128)(2,1)}, u32[]{:S(2)}) copy-start(bf16[1,3,1280,80]{2,3,1,0:T(8,128)(2,1)} %get-tuple-element.50) | copy-start | bytes 1843204
  95.5 2.7 %copy-start.2 = (bf16[1,1,32,72,1280]{4,3,1,0,2:T(8,128)(2,1)S(1)}, bf16[1,1,32,72,1280]{4,3,1,0,2:T(8,128)(2,1)}, u32[]{:S(2)}) copy-start(bf16[1,1,32,72,1280]{4,3,1,0,2:T(8,128)(2,1)} %multiply_convert_fusion) | copy-start | bytes 17694724
  95.5 2.8 %copy-start.5 = (bf16[1,3,1280,80]{2,3,1,0:T(8,128)(2,1)S(1)}, bf16[1,3,1280,80]{2,3,1,0:T(8,128)(2,1)}, u32[]{:S(2)}) copy-start(bf16[1,3,1280,80]{2,3,1,0:T(8,128)(2,1)} %get-tuple-element.51) | copy-start | bytes 1843204
  107.1 19.6 %copy-start.6 = (bf16[1,1,2,72,1280]{4,3,2,1,0:T(8,128)(2,1)S(1)}, bf16[1,1,2,72,1280]{4,3,2,1,0:T(8,128)(2,1)}, u32[]{:S(2)}) copy-start(bf16[1,1,2,72,1280]{4,3,2,1,0:T(8,128)(2,1)} %param.13) | copy-start | bytes 1105924
  107.1 19.6 %copy-start.9 = (f32[1280]{0:T(1024)S(1)}, f32[1280]{0:T(1024)}, u32[]{:S(2)}) copy-start(f32[1280]{0:T(1024)} %param.21) | copy-start | bytes 15364
  110.0 17.2 %copy-start.10 = (f32[1280]{0:T(1024)S(1)}, f32[1280]{0:T(1024)}, u32[]{:S(2)}) copy-start(f32[1280]{0:T(1024)} %param.22) | copy-start | bytes 15364
  110.8 76.9 %copy-start.13 = (f32[20]{0:T(128)S(1)}, f32[20]{0:T(128)}, u32[]{:S(2)}) copy-start(f32[20]{0:T(128)} %param.25) | copy-start | bytes 244
  184.4 11.5 %collective-permute-start = (bf16[16,3,640,80]{2,3,1,0:T(8,128)(2,1)}, bf16[16,3,640,80]{2,3,1,0:T(8,128)(2,1)}, u32[]{:S(2)}, u32[]{:S(2)}) collective-permute-start(bf16[16,3,640,80]{2,3,1,0:T(8,128)(2,1)} %bitcast.91), channel_id=1, source_target_pairs={{0,1},{1,0},{2,3},{3,2},{4,5},{5,4},{6,7},{7,6},{8,9},{9,8},{10,11... | collective-permute-start | bytes 14745608 | tf_op jit(solution)/shard_map/ppermute | solution.py:123
  203.4 4.7 %copy-start.7 = (bf16[16,9,20,64]{3,2,1,0:T(8,128)(2,1)S(1)}, bf16[16,9,20,64]{3,2,1,0:T(8,128)(2,1)}, u32[]{:S(2)}) copy-start(bf16[16,9,20,64]{3,2,1,0:T(8,128)(2,1)} %reshape_squeeze.10) | copy-start | bytes 1105924
  211.3 29.6 %copy-start.4 = (bf16[16,80,640]{2,1,0:T(8,128)(2,1)S(1)}, bf16[16,80,640]{2,1,0:T(8,128)(2,1)}, u32[]{:S(2)}) copy-start(bf16[16,80,640]{2,1,0:T(8,128)(2,1)} %copy-done.3) | copy-start | bytes 4915204
  213.5 35.4 %copy-start.1 = (bf16[3,1280,80]{1,2,0:T(8,128)(2,1)S(1)}, bf16[3,1280,80]{1,2,0:T(8,128)(2,1)}, u32[]{:S(2)}) copy-start(bf16[3,1280,80]{1,2,0:T(8,128)(2,1)} %param.23) | copy-start | bytes 1843204
  240.9 5.3 %collective-permute-start.1 = (bf16[1280,640]{1,0:T(8,128)(2,1)S(1)}, bf16[1280,640]{1,0:T(8,128)(2,1)}, u32[]{:S(2)}, u32[]{:S(2)}) collective-permute-start(bf16[1280,640]{1,0:T(8,128)(2,1)S(1)} %bitcast.93), channel_id=1, source_target_pairs={{0,1},{1,0},{2,3},{3,2},{4,5},{5,4},{6,7},{7,6},{8,9},{9,8},{10,11... | collective-permute-start | bytes 4915208 | tf_op jit(solution)/shard_map/ppermute | solution.py:135
Sparse Core Ops, SparseCore 0:
  9.2 62.6 all-gather.3
  74.5 109.8 all-gather.5

commit v2 on v1

--- a/solution.py
+++ b/solution.py
@@ -34,7 +34,23 @@
 
 
 def send_back(mixed):
-    return lax.all_to_all(mixed, VIEW, split_axis=0, concat_axis=1, tiled=True)
+    ys = lax.axis_size("vy")
+    zs = lax.axis_size("vz")
+    parts = mixed.reshape((zs, ys) + mixed.shape[1:])
+    parts = lax.all_to_all(parts, "vy", split_axis=1, concat_axis=1, tiled=True)
+    parts = lax.all_to_all(parts, "vz", split_axis=0, concat_axis=0, tiled=True)
+    return jnp.moveaxis(parts.reshape(mixed.shape), 0, 1)
+
+
+def send_out(pixel_major):
+    ys = lax.axis_size("vy")
+    zs = lax.axis_size("vz")
+    local_views = pixel_major.shape[0]
+    parts = pixel_major.reshape((local_views, zs, ys) + pixel_major.shape[2:])
+    parts = lax.all_to_all(parts, "vy", split_axis=2, concat_axis=0, tiled=True)
+    parts = lax.all_to_all(parts, "vz", split_axis=1, concat_axis=1, tiled=True)
+    parts = jnp.swapaxes(parts, 0, 1)
+    return parts.reshape((zs * ys * local_views, 1) + pixel_major.shape[2:])
 
 
 def local(
@@ -117,7 +133,7 @@
     pixel_major = jnp.moveaxis(normed_y, 1, 0).reshape(
         local_views, view_devices, per_device, width_out
     )
-    views = lax.all_to_all(pixel_major, VIEW, split_axis=1, concat_axis=0, tiled=True)
+    views = send_out(pixel_major)
     in_half, views = lax.optimization_barrier((in_half, views))
     swap = [(0, 1), (1, 0)]
     in_other = lax.ppermute(in_half, "core", swap)

time: 257 us -> 255 us (level)
  waiting for transfers between devices: 76.4 us -> 70.1 us
  blocking collectives: 72.1 us -> 76.1 us
    all_gather x1, waiting for transfers between devices: 25.6 us -> 20.3 us  [local(): in_half = lax.all_gather(in_half, VIEW, axis=0, tiled=False)]
    all_to_all x2 -> x4, blocking collectives: 56.8 us -> 60.6 us  [the longest x1 18.5 us: send_out(): parts = lax.all_to_all(parts, 'vz', split_axis=1, concat_axis=1, tiled=True)]
  transfers between devices with their start and end apart: 5 -> 5, of which waited for: 4 -> 4; matrix products, arithmetic and copies ran while one was open for 20% -> 21% of each run, Pallas kernels for 0% -> 0%
where the time goes in v2:
time: 255 us
  blocking collectives  76.1 us (30%)
  waiting for transfers between devices  70.1 us (27%)
  local copies, waits for them, and re-layouts  30.7 us (12%)
  matrix products  22.9 us (9%)
  other arithmetic  22 us (9%)
  starting transfers between devices  17.9 us (7%)
  between operations  15.1 us (6%)
    all_gather x1, waiting for transfers between devices, local(): whole = lax.all_gather(latent, ROW, axis=2, tiled=True)  45.7 us
    all_gather x1, waiting for transfers between devices, local(): in_half = lax.all_gather(in_half, VIEW, axis=0, tiled=False)  20.3 us
    all_to_all x1, blocking collectives, send_out(): parts = lax.all_to_all(parts, 'vz', split_axis=1, concat_axis=1, tiled=True)  18.5 us
    all_to_all x1, blocking collectives, send_back(): parts = lax.all_to_all(parts, 'vz', split_axis=0, concat_axis=0, tiled=True)  16.4 us
    all_to_all x1, blocking collectives, send_out(): parts = lax.all_to_all(parts, 'vy', split_axis=2, concat_axis=0, tiled=True)  15.8 us
    all_to_all x1, blocking collectives, local(): lax.all_to_all(conv_part, ROW, split_axis=2, concat_axis=4, tiled=True)  15.4 us
    all_to_all x1, starting transfers between devices, local(): lax.all_to_all(out_half, VIEW, split_axis=0, concat_axis=0, tiled=True)  11.7 us
    all_to_all x1, blocking collectives, send_back(): parts = lax.all_to_all(parts, 'vy', split_axis=1, concat_axis=1, tiled=True)  9.96 us
  transfers between devices with their start and end apart: 5, of which 4 were waited for; matrix products, arithmetic and copies ran while one was open for 21% of the time, Pallas kernels for 0%

profile of v2, /device:TPU:1, one launch (start us, length us, event | category | flops | bytes accessed | tf_op | source)
XLA Modules:
  0.0 254.7 jit_solution(4263737149790404709)
XLA Ops:
  8.2 1.3 broadcast_in_dim.26
  9.5 11.7 %all-to-all-start = ((bf16[16,80,640]{2,1,0:T(8,128)(2,1)}), bf16[16,80,640]{2,1,0:T(8,128)(2,1)S(1)}, u32[]{:S(2)}, u32[]{:S(2)}) async-start(bf16[16,80,640]{2,1,0:T(8,128)(2,1)} %broadcast_in_dim.26), calls=%async_computation | async-start | bytes 3276800 | tf_op jit(solution)/shard_map/all_to_all | solution.py:84
  23.5 2.6 %fusion.52 = (bf16[1,3,1280,80]{2,3,1,0:T(8,128)(2,1)S(1)}, bf16[1,3,1280,80]{2,3,1,0:T(8,128)(2,1)}, bf16[1,3,1280,80]{2,3,1,0:T(8,128)(2,1)}) fusion(bf16[3,3,1280,80]{2,3,1,0:T(8,128)(2,1)} %param.20), kind=kLoop, calls=%fused_computation.74 | loop fusion | bytes 3686400 | tf_op jit(solution)/shard_map/slice | solution.py:109
  26.1 45.7 %all-gather.4.cloned.1.call-done = bf16[1,1,32,72,1280]{4,3,1,0,2:T(8,128)(2,1)} async-done(((bf16[1,1,2,72,1280]{4,3,1,0,2:T(8,128)(2,1)}), bf16[1,1,32,72,1280]{4,3,1,0,2:T(8,128)(2,1)}) %all-gather.4.cloned.1.call-update) | async-done | bytes 5898256 | tf_op jit(solution)/shard_map/all_gather | solution.py:74
  71.9 3.5 %convert_reduce_fusion = f32[1280]{0:T(1024)S(1)} fusion(bf16[1,1,32,72,1280]{4,3,1,0,2:T(8,128)(2,1)} %all-gather.4.cloned.1.call-done), kind=kLoop, calls=%fused_computation.2 | loop fusion | flops 5896960 | bytes 5903360 | tf_op jit(solution)/shard_map/reduce_sum | solution.py:92
  76.6 4.3 %fusion.3 = f32[1280]{0:T(1024)S(1)} fusion(bf16[1,1,32,72,1280]{4,3,1,0,2:T(8,128)(2,1)} %all-gather.4.cloned.1.call-done, f32[1280]{0:T(1024)S(1)} %sub.42), kind=kLoop, calls=%fused_computation.5 | loop fusion | flops 11795200 | bytes 5908480 | tf_op jit(solution)/shard_map/reduce_sum | solution.py:94
  81.2 8.5 %multiply_convert_fusion = bf16[1,1,32,72,1280]{4,3,1,0,2:T(8,128)(2,1)} fusion(bf16[1,1,32,72,1280]{4,3,1,0,2:T(8,128)(2,1)} %all-gather.4.cloned.1.call-done, f32[1280]{0:T(1024)S(1)} %get-tuple-element.44, f32[1280]{0:T(1024)S(1)} %get-tuple-element.43, f32[1280]{0:T(1024)S(1)} %copy-done.11, f32[1280]{0:T(1024)S(1)} %copy-done.12, f32[1280]{0:T(1024)S(1)} %mul.83, ...), kind=kLoop, calls=%fused_computation.10 | loop fusion | flops 35389440 | bytes 11827200 | tf_op jit(solution)/shard_map/convert_element_type | solution.py:102
  89.8 5.6 %pad_slice_fusion = (bf16[1,1,32,72,1280]{4,3,1,0,2:T(8,128)(2,1)S(1)}, bf16[1,1,32,72,1280]{4,3,1,0,2:T(8,128)(2,1)S(1)}) fusion(bf16[1,1,32,72,1280]{4,3,1,0,2:T(8,128)(2,1)} %multiply_convert_fusion), kind=kLoop, calls=%fused_computation.11 | loop fusion | bytes 17694720 | tf_op jit(solution)/shard_map/slice | solution.py:108
  95.4 1.7 fusion.59
  98.2 1.8 convolution_add_fusion.1
  100.0 1.8 convolution_add_fusion
  101.8 5.2 %reshape.313 = f32[1,1,32,72,3,80]{3,2,5,4,1,0:T(8,128)} reshape(f32[2304,240]{0,1:T(8,128)S(1)} %convolution_add_fusion) | data formatting | bytes 4423680 | tf_op jit(solution)/shard_map/reshape | solution.py:112
  107.1 2.9 %fusion.35 = bf16[1,1,32,72,80]{3,2,4,1,0:T(8,128)(2,1)S(1)} fusion(f32[1,1,32,72,3,80]{3,2,5,4,1,0:T(8,128)} %reshape.313), kind=kLoop, calls=%fused_computation.50 | loop fusion | flops 552960 | bytes 5611520 | tf_op jit(solution)/shard_map/convert_element_type | solution.py:120
  110.7 15.4 %all_to_all.47 = bf16[1,1,32,72,80]{4,3,1,0,2:T(8,128)(2,1)S(1)} all-to-all(bf16[1,1,32,72,80]{4,3,1,0,2:T(8,128)(2,1)S(1)} %copy.61), channel_id=1, replica_groups=mesh['vz'=8,'vy'=2,'chip'=8,'core'=2] {'chip','core'}, dimensions={2} | all-to-all | bytes 737280 | tf_op jit(solution)/shard_map/all_to_all | solution.py:121
  128.1 15.8 %all_to_all.48 = bf16[1,8,2,9,1280]{4,1,3,0,2:T(8,128)(2,1)S(1)} all-to-all(bf16[1,8,2,9,1280]{4,1,3,0,2:T(8,128)(2,1)S(1)} %copy.63), channel_id=1, replica_groups=mesh['vz'=8,'vy'=2,'chip'=8,'core'=2] {'vy'}, dimensions={2} | all-to-all | bytes 737280 | tf_op jit(solution)/shard_map/all_to_all | solution.py:50
  144.1 18.5 %all_to_all.49 = bf16[2,8,1,9,1280]{4,0,3,2,1:T(2,128)(2,1)S(1)} all-to-all(bf16[2,8,1,9,1280]{4,0,3,2,1:T(2,128)(2,1)S(1)} %copy.64), channel_id=1, replica_groups=mesh['vz'=8,'vy'=2,'chip'=8,'core'=2] {'vz'}, dimensions={1} | all-to-all | bytes 737280 | tf_op jit(solution)/shard_map/all_to_all | solution.py:51
  163.0 20.3 %all-gather.6.cloned.1.call-done = bf16[48,640,80]{1,2,0:T(8,128)(2,1)} async-done(((bf16[3,640,80]{1,2,0:T(8,128)(2,1)}), bf16[48,640,80]{1,2,0:T(8,128)(2,1)}) %all-gather.6.cloned.1.call-update) | async-done | bytes 4915216 | tf_op jit(solution)/shard_map/all_gather | solution.py:80
  183.4 3.2 %collective-permute-start = (bf16[16,3,640,80]{2,3,1,0:T(8,128)(2,1)}, bf16[16,3,640,80]{2,3,1,0:T(8,128)(2,1)}, u32[]{:S(2)}, u32[]{:S(2)}) collective-permute-start(bf16[16,3,640,80]{2,3,1,0:T(8,128)(2,1)} %bitcast.100), channel_id=1, source_target_pairs={{0,1},{1,0},{2,3},{3,2},{4,5},{5,4},{6,7},{7,6},{8,9},{9,8},{10,11... | collective-permute-start | bytes 14745608 | tf_op jit(solution)/shard_map/ppermute | solution.py:139
  186.9 5.1 %fusion.37 = f32[16,3,80,144]{2,3,1,0:T(8,128)S(1)} fusion(bf16[16,3,640,80]{2,3,1,0:T(8,128)(2,1)} %bitcast.101, bf16[144,1280]{1,0:T(8,128)(2,1)S(1)} %reshape.315, s32[]{:T(128)S(6)} %select_n.60), kind=kOutput, calls=%fused_computation.52 | convolution fusion | flops 707788800 | bytes 7311364 | tf_op jit(solution)/shard_map/pc,jmcd->mpjd/dot_general | solution.py:143
  192.0 2.8 %collective-permute-done = bf16[16,3,640,80]{2,3,1,0:T(8,128)(2,1)} collective-permute-done((bf16[16,3,640,80]{2,3,1,0:T(8,128)(2,1)}, bf16[16,3,640,80]{2,3,1,0:T(8,128)(2,1)}, u32[]{:S(2)}, u32[]{:S(2)}) %collective-permute-start) | collective-permute-done | bytes 4915232 | tf_op jit(solution)/shard_map/ppermute | solution.py:139
  194.7 5.1 %fusion.13 = bf16[3,144,16,80]{3,1,0,2:T(8,128)(2,1)S(1)} fusion(f32[16,3,80,144]{2,3,1,0:T(8,128)S(1)} %fusion.37, bf16[16,3,640,80]{2,3,1,0:T(8,128)(2,1)} %collective-permute-done, bf16[144,1280]{1,0:T(8,128)(2,1)S(1)} %reshape.315, s32[]{:T(128)S(6)} %select_n.66), kind=kOutput, calls=%fused_computation.23 | convolution fusion | flops 708894720 | bytes 9744388 | tf_op jit(solution)/shard_map/pc,jmcd->mpjd/dot_general | solution.py:145
  200.1 2.2 reshape_squeeze.10
  202.5 2.2 reshape_squeeze.11
  204.9 1.3 reshape_squeeze.9
  206.1 3.2 %fusion.54 = (f32[9,20,16]{2,1,0:T(8,128)S(1)}, f32[9,20,16,16]{2,3,1,0:T(8,128)}) fusion(bf16[16,9,20,64]{3,2,1,0:T(8,128)(2,1)} %reshape_squeeze.11, bf16[16,9,20,64]{3,2,1,0:T(8,128)(2,1)S(1)} %copy-done.7, f32[20]{0:T(128)S(1)} %broadcast_multiply_fusion.1), kind=kOutput, calls=%fused_computation.76 | convolution fusion | flops 6036495 | bytes 933200 | tf_op jit(solution)/shard_map/sub | solution.py:28
  209.3 1.8 fusion.18
  211.9 10.0 %all_to_all.50 = bf16[8,2,1,9,1280]{4,0,3,2,1:T(8,128)(2,1)S(1)} all-to-all(bf16[8,2,1,9,1280]{4,0,3,2,1:T(8,128)(2,1)S(1)} %copy.75), channel_id=1, replica_groups=mesh['vz'=8,'vy'=2,'chip'=8,'core'=2] {'vy'}, dimensions={1} | all-to-all | bytes 737280 | tf_op jit(solution)/shard_map/all_to_all | solution.py:40
  222.2 16.4 %all_to_all.51 = bf16[8,2,1,9,1280]{4,1,3,2,0:T(2,128)(2,1)S(1)} all-to-all(bf16[8,2,1,9,1280]{4,1,3,2,0:T(2,128)(2,1)S(1)} %copy.76), channel_id=1, replica_groups=mesh['vz'=8,'vy'=2,'chip'=8,'core'=2] {'vz'}, dimensions={0} | all-to-all | bytes 737280 | tf_op jit(solution)/shard_map/all_to_all | solution.py:41
  239.0 2.8 %collective-permute-start.1 = (bf16[1280,640]{1,0:T(8,128)(2,1)S(1)}, bf16[1280,640]{1,0:T(8,128)(2,1)}, u32[]{:S(2)}, u32[]{:S(2)}) collective-permute-start(bf16[1280,640]{1,0:T(8,128)(2,1)S(1)} %bitcast.102), channel_id=1, source_target_pairs={{0,1},{1,0},{2,3},{3,2},{4,5},{5,4},{6,7},{7,6},{8,9},{9,8},{10,11... | collective-permute-start | bytes 4915208 | tf_op jit(solution)/shard_map/ppermute | solution.py:151
  241.8 1.0 copy.78
  242.8 1.3 reshape.316
  245.1 1.9 fusion.22
  (76 shorter events, 12.6 us)
Async XLA Ops:
  6.5 69.0 %copy-start = (bf16[3,1280,80]{1,2,0:T(8,128)(2,1)S(1)}, bf16[3,1280,80]{1,2,0:T(8,128)(2,1)}, u32[]{:S(2)}) copy-start(bf16[3,1280,80]{1,2,0:T(8,128)(2,1)} %param.23) | copy-start | bytes 1843204
  6.5 65.3 %all-gather.4.cloned.1.call-start = ((), (), s32[]{:S(2)}) async-start(), calls=%async_computation.6 | async-start | bytes 6266880 | tf_op jit(solution)/shard_map/all_gather | solution.py:74
  9.5 80.3 %all-to-all-start = ((bf16[16,80,640]{2,1,0:T(8,128)(2,1)}), bf16[16,80,640]{2,1,0:T(8,128)(2,1)S(1)}, u32[]{:S(2)}, u32[]{:S(2)}) async-start(bf16[16,80,640]{2,1,0:T(8,128)(2,1)} %broadcast_in_dim.26), calls=%async_computation | async-start | bytes 3276800 | tf_op jit(solution)/shard_map/all_to_all | solution.py:84
  21.3 162.1 %all-gather.6.cloned.1.call-start = ((), (), s32[]{:S(2)}) async-start(), calls=%async_computation.7 | async-start | bytes 5222400 | tf_op jit(solution)/shard_map/all_gather | solution.py:80
  75.4 5.8 %copy-start.11 = (f32[1280]{0:T(1024)S(1)}, f32[1280]{0:T(1024)}, u32[]{:S(2)}) copy-start(f32[1280]{0:T(1024)} %param.15) | copy-start | bytes 15364
  75.4 5.8 %copy-start.12 = (f32[1280]{0:T(1024)S(1)}, f32[1280]{0:T(1024)}, u32[]{:S(2)}) copy-start(f32[1280]{0:T(1024)} %param.14) | copy-start | bytes 15364
  89.8 5.6 %copy-start.3 = (bf16[16,80,640]{2,1,0:T(8,128)(2,1)}, bf16[16,80,640]{2,1,0:T(8,128)(2,1)S(1)}, u32[]{:S(2)}) copy-start(bf16[16,80,640]{2,1,0:T(8,128)(2,1)S(1)} %all-to-all-done) | copy-start | bytes 4915204
  89.8 5.6 %copy-start.8 = (bf16[1,3,1280,80]{2,3,1,0:T(8,128)(2,1)S(1)}, bf16[1,3,1280,80]{2,3,1,0:T(8,128)(2,1)}, u32[]{:S(2)}) copy-start(bf16[1,3,1280,80]{2,3,1,0:T(8,128)(2,1)} %get-tuple-element.50) | copy-start | bytes 1843204
  95.4 2.7 %copy-start.2 = (bf16[1,1,32,72,1280]{4,3,1,0,2:T(8,128)(2,1)S(1)}, bf16[1,1,32,72,1280]{4,3,1,0,2:T(8,128)(2,1)}, u32[]{:S(2)}) copy-start(bf16[1,1,32,72,1280]{4,3,1,0,2:T(8,128)(2,1)} %multiply_convert_fusion) | copy-start | bytes 17694724
  95.4 2.8 %copy-start.5 = (bf16[1,3,1280,80]{2,3,1,0:T(8,128)(2,1)S(1)}, bf16[1,3,1280,80]{2,3,1,0:T(8,128)(2,1)}, u32[]{:S(2)}) copy-start(bf16[1,3,1280,80]{2,3,1,0:T(8,128)(2,1)} %get-tuple-element.51) | copy-start | bytes 1843204
  107.1 19.8 %copy-start.6 = (bf16[1,1,2,72,1280]{4,3,2,1,0:T(8,128)(2,1)S(1)}, bf16[1,1,2,72,1280]{4,3,2,1,0:T(8,128)(2,1)}, u32[]{:S(2)}) copy-start(bf16[1,1,2,72,1280]{4,3,2,1,0:T(8,128)(2,1)} %param.13) | copy-start | bytes 1105924
  107.1 19.8 %copy-start.9 = (f32[1280]{0:T(1024)S(1)}, f32[1280]{0:T(1024)}, u32[]{:S(2)}) copy-start(f32[1280]{0:T(1024)} %param.21) | copy-start | bytes 15364
  110.0 17.4 %copy-start.10 = (f32[1280]{0:T(1024)S(1)}, f32[1280]{0:T(1024)}, u32[]{:S(2)}) copy-start(f32[1280]{0:T(1024)} %param.22) | copy-start | bytes 15364
  126.3 60.3 %copy-start.13 = (f32[20]{0:T(128)S(1)}, f32[20]{0:T(128)}, u32[]{:S(2)}) copy-start(f32[20]{0:T(128)} %param.25) | copy-start | bytes 244
  183.4 11.4 %collective-permute-start = (bf16[16,3,640,80]{2,3,1,0:T(8,128)(2,1)}, bf16[16,3,640,80]{2,3,1,0:T(8,128)(2,1)}, u32[]{:S(2)}, u32[]{:S(2)}) collective-permute-start(bf16[16,3,640,80]{2,3,1,0:T(8,128)(2,1)} %bitcast.100), channel_id=1, source_target_pairs={{0,1},{1,0},{2,3},{3,2},{4,5},{5,4},{6,7},{7,6},{8,9},{9,8},{10,11... | collective-permute-start | bytes 14745608 | tf_op jit(solution)/shard_map/ppermute | solution.py:139
  202.3 3.8 %copy-start.7 = (bf16[16,9,20,64]{3,2,1,0:T(8,128)(2,1)S(1)}, bf16[16,9,20,64]{3,2,1,0:T(8,128)(2,1)}, u32[]{:S(2)}) copy-start(bf16[16,9,20,64]{3,2,1,0:T(8,128)(2,1)} %reshape_squeeze.10) | copy-start | bytes 1105924
  211.1 27.8 %copy-start.4 = (bf16[16,80,640]{2,1,0:T(8,128)(2,1)S(1)}, bf16[16,80,640]{2,1,0:T(8,128)(2,1)}, u32[]{:S(2)}) copy-start(bf16[16,80,640]{2,1,0:T(8,128)(2,1)} %copy-done.3) | copy-start | bytes 4915204
  222.2 25.7 %copy-start.1 = (bf16[3,1280,80]{1,2,0:T(8,128)(2,1)S(1)}, bf16[3,1280,80]{1,2,0:T(8,128)(2,1)}, u32[]{:S(2)}) copy-start(bf16[3,1280,80]{1,2,0:T(8,128)(2,1)} %param.23) | copy-start | bytes 1843204
  239.0 6.1 %collective-permute-start.1 = (bf16[1280,640]{1,0:T(8,128)(2,1)S(1)}, bf16[1280,640]{1,0:T(8,128)(2,1)}, u32[]{:S(2)}, u32[]{:S(2)}) collective-permute-start(bf16[1280,640]{1,0:T(8,128)(2,1)S(1)} %bitcast.102), channel_id=1, source_target_pairs={{0,1},{1,0},{2,3},{3,2},{4,5},{5,4},{6,7},{7,6},{8,9},{9,8},{10,11... | collective-permute-start | bytes 4915208 | tf_op jit(solution)/shard_map/ppermute | solution.py:151
Sparse Core Ops, SparseCore 0:
  9.2 62.6 all-gather.3
  76.4 106.9 all-gather.5

commit v3 on v2

--- a/solution.py
+++ b/solution.py
@@ -77,12 +77,12 @@
     half_in = attn_in.shape[1] // 2
     half_out = attn_out.shape[1] // 2
     in_half = lax.dynamic_slice_in_dim(attn_in, core * half_in, half_in, axis=1)
-    in_half = lax.all_gather(in_half, VIEW, axis=0, tiled=False)
     out_half = lax.dynamic_slice_in_dim(attn_out, core * half_out, half_out, axis=1)
+    packed = jnp.concatenate([in_half.reshape(-1), out_half.reshape(-1)])
+    packed = lax.all_gather(packed, VIEW, axis=0, tiled=False)
     view_devices = lax.axis_size(VIEW)
-    out_half = jnp.broadcast_to(out_half[None], (view_devices,) + out_half.shape)
-    out_half = lax.all_to_all(out_half, VIEW, split_axis=0, concat_axis=0, tiled=True)
-    out_half = out_half.reshape(-1, half_out)
+    out_half = packed[:, in_half.size :].reshape(-1, half_out)
+    in_half = packed[:, : in_half.size].reshape((view_devices,) + in_half.shape)
 
     all_rows = whole.shape[2]
     x_float = whole.astype(jnp.float32)
@@ -100,7 +100,6 @@
     film_shift = film_rows[:, :, None, None, channels:]
     hidden = (normed * gn_gain + gn_bias) * (1.0 + film_scale) + film_shift
     activated = jax.nn.silu(hidden).astype(jnp.bfloat16)
-    out_half, activated = lax.optimization_barrier((out_half, activated))
     taps = conv_w.shape[1]
     padded = jnp.pad(activated, ((0, 0), (0, 0), (1, 1), (0, 0), (0, 0)))
     tap_sum = None

time: 255 us -> 285 us (1.12)
  waiting for transfers between devices: 70.1 us -> 100 us
  local copies, waits for them, and re-layouts: 30.7 us -> 55.5 us
  blocking collectives: 76.1 us -> 59.5 us
  starting transfers between devices: 17.9 us -> 8.51 us
    all_to_all x1 -> x0, blocking collectives: 16.4 us -> none  [send_back(): parts = lax.all_to_all(parts, 'vz', split_axis=0, concat_axis=0, tiled=True)]
    all_gather x1, waiting for transfers between devices: 20.3 us -> 36.1 us  [local(): packed = lax.all_gather(packed, VIEW, axis=0, tiled=False)]
    reshape x0 -> x4, local copies, waits for them, and re-layouts: none -> 14.9 us  [the longest x1 12.3 us: local(): in_half = packed[:, :in_half.size].reshape((view_devices,) + in_half.shape)]
    all_to_all x1, waiting for transfers between devices: 0.01 us -> 10.4 us  [send_back(): parts = lax.all_to_all(parts, 'vz', split_axis=0, concat_axis=0, tiled=True)]
    optimization_barrier x1 -> x2, local copies, waits for them, and re-layouts: 0.13 us -> 9.7 us  [local(): in_half, views = lax.optimization_barrier((in_half, views))]
    all_to_all x1, starting transfers between devices: 11.7 us -> 4.23 us  [send_back(): parts = lax.all_to_all(parts, 'vz', split_axis=0, concat_axis=0, tiled=True)]
    all_gather x0 -> x1, local copies, waits for them, and re-layouts: none -> 6.47 us  [local(): packed = lax.all_gather(packed, VIEW, axis=0, tiled=False)]
    slice x1, local copies, waits for them, and re-layouts: 5.61 us -> 0.83 us  [local(): rows_in = padded[:, :, tap_row:tap_row + all_rows].reshape(-1, channels)]
  transfers between devices with their start and end apart: 5 -> 5, of which waited for: 4 -> 5; matrix products, arithmetic and copies ran while one was open for 21% -> 16% of each run, Pallas kernels for 0% -> 0%
where the time goes in v3:
time: 285 us; the launch traced here: 284 us
  waiting for transfers between devices  100 us (35%)
  blocking collectives  59.5 us (21%)
  local copies, waits for them, and re-layouts  55.5 us (19%)
  matrix products  24.1 us (8%)
  other arithmetic  21 us (7%)
  between operations  15.1 us (5%)
  starting transfers between devices  8.51 us (3%)
    all_gather x1, waiting for transfers between devices, local(): whole = lax.all_gather(latent, ROW, axis=2, tiled=True)  48.7 us
    all_gather x1, waiting for transfers between devices, local(): packed = lax.all_gather(packed, VIEW, axis=0, tiled=False)  36.1 us
    all_to_all x1, blocking collectives, send_out(): parts = lax.all_to_all(parts, 'vz', split_axis=1, concat_axis=1, tiled=True)  18.5 us
    all_to_all x1, blocking collectives, send_out(): parts = lax.all_to_all(parts, 'vy', split_axis=2, concat_axis=0, tiled=True)  15.5 us
    all_to_all x1, blocking collectives, local(): lax.all_to_all(conv_part, ROW, split_axis=2, concat_axis=4, tiled=True)  15.5 us
    reshape x1, local copies, waits for them, and re-layouts, local(): in_half = packed[:, :in_half.size].reshape((view_devices,) + in_half.shape)  12.3 us
    all_to_all x1, waiting for transfers between devices, send_back(): parts = lax.all_to_all(parts, 'vz', split_axis=0, concat_axis=0, tiled=True)  10.4 us
    all_to_all x1, blocking collectives, send_back(): parts = lax.all_to_all(parts, 'vy', split_axis=1, concat_axis=1, tiled=True)  9.97 us
  transfers between devices with their start and end apart: 5, of which 5 were waited for; matrix products, arithmetic and copies ran while one was open for 16% of the time, Pallas kernels for 0%

profile of v3, /device:TPU:1, one launch (start us, length us, event | category | flops | bytes accessed | tf_op | source)
XLA Modules:
  0.0 283.8 jit_solution(5268199768287122619)
XLA Ops:
  8.3 48.7 %all-gather.4.cloned.1.call-done = bf16[1,1,32,72,1280]{4,3,1,0,2:T(8,128)(2,1)} async-done(((bf16[1,1,2,72,1280]{4,3,1,0,2:T(8,128)(2,1)}), bf16[1,1,32,72,1280]{4,3,1,0,2:T(8,128)(2,1)}) %all-gather.4.cloned.1.call-update) | async-done | bytes 5898256 | tf_op jit(solution)/shard_map/all_gather | solution.py:74
  62.2 3.6 %convert_reduce_fusion = f32[1280]{0:T(1024)S(1)} fusion(bf16[1,1,32,72,1280]{4,3,1,0,2:T(8,128)(2,1)} %all-gather.4.cloned.1.call-done), kind=kLoop, calls=%fused_computation.2 | loop fusion | flops 5896960 | bytes 5903360 | tf_op jit(solution)/shard_map/reduce_sum | solution.py:92
  66.1 4.3 %fusion.3 = f32[1280]{0:T(1024)S(1)} fusion(bf16[1,1,32,72,1280]{4,3,1,0,2:T(8,128)(2,1)} %all-gather.4.cloned.1.call-done, f32[1280]{0:T(1024)S(1)} %sub.42), kind=kLoop, calls=%fused_computation.5 | loop fusion | flops 11795200 | bytes 5908480 | tf_op jit(solution)/shard_map/reduce_sum | solution.py:94
  70.8 6.7 %multiply_convert_fusion = bf16[1,1,32,72,1280]{4,3,1,0,2:T(8,128)(2,1)S(1)} fusion(bf16[1,1,32,72,1280]{4,3,1,0,2:T(8,128)(2,1)} %all-gather.4.cloned.1.call-done, f32[1280]{0:T(1024)S(1)} %get-tuple-element.40, f32[1280]{0:T(1024)S(1)} %get-tuple-element.39, f32[1280]{0:T(1024)S(1)} %copy-done.8, f32[1280]{0:T(1024)S(1)} %copy-done.9, f32[1280]{0:T(1024)S(1)} %mul.82, ...), kind=kLoop, calls=%fused_computation.10 | loop fusion | flops 35389440 | bytes 11827200 | tf_op jit(solution)/shard_map/convert_element_type | solution.py:102
  78.5 1.7 fusion.59
  80.3 1.8 convolution_add_fusion.1
  82.1 1.8 convolution_add_fusion
  83.9 5.3 %reshape.320 = f32[1,1,32,72,3,80]{3,2,5,4,1,0:T(8,128)} reshape(f32[2304,240]{0,1:T(8,128)S(1)} %convolution_add_fusion) | data formatting | bytes 4423680 | tf_op jit(solution)/shard_map/reshape | solution.py:111
  89.2 2.9 %fusion.35 = bf16[1,1,32,72,80]{3,2,4,1,0:T(8,128)(2,1)S(1)} fusion(f32[1,1,32,72,3,80]{3,2,5,4,1,0:T(8,128)} %reshape.320), kind=kLoop, calls=%fused_computation.50 | loop fusion | flops 552960 | bytes 5611520 | tf_op jit(solution)/shard_map/convert_element_type | solution.py:119
  92.9 15.5 %all_to_all.42 = bf16[1,1,32,72,80]{4,3,1,0,2:T(8,128)(2,1)S(1)} all-to-all(bf16[1,1,32,72,80]{4,3,1,0,2:T(8,128)(2,1)S(1)} %copy.70), channel_id=1, replica_groups=mesh['vz'=8,'vy'=2,'chip'=8,'core'=2] {'chip','core'}, dimensions={2} | all-to-all | bytes 737280 | tf_op jit(solution)/shard_map/all_to_all | solution.py:120
  110.3 15.5 %all_to_all.43 = bf16[1,8,2,9,1280]{4,1,3,0,2:T(8,128)(2,1)S(1)} all-to-all(bf16[1,8,2,9,1280]{4,1,3,0,2:T(8,128)(2,1)S(1)} %copy.73), channel_id=1, replica_groups=mesh['vz'=8,'vy'=2,'chip'=8,'core'=2] {'vy'}, dimensions={2} | all-to-all | bytes 737280 | tf_op jit(solution)/shard_map/all_to_all | solution.py:50
  126.1 18.5 %all_to_all.44 = bf16[2,8,1,9,1280]{4,0,3,2,1:T(2,128)(2,1)S(1)} all-to-all(bf16[2,8,1,9,1280]{4,0,3,2,1:T(2,128)(2,1)S(1)} %copy.74), channel_id=1, replica_groups=mesh['vz'=8,'vy'=2,'chip'=8,'core'=2] {'vz'}, dimensions={1} | all-to-all | bytes 737280 | tf_op jit(solution)/shard_map/all_to_all | solution.py:51
  145.0 36.1 %all-gather.6.cloned.1.call-done = bf16[3276800]{0:T(1024)(128)(2,1)} async-done(((bf16[204800]{0:T(1024)(128)(2,1)}), bf16[3276800]{0:T(1024)(128)(2,1)}) %all-gather.6.cloned.1.call-update) | async-done | bytes 6553616 | tf_op jit(solution)/shard_map/all_gather | solution.py:82
  181.0 6.5 %reshape.388 = bf16[16,204800]{1,0:T(8,128)(2,1)} reshape(bf16[3276800]{0:T(1024)(128)(2,1)} %all-gather.6.cloned.1.call-done) | data formatting | bytes 13107200 | tf_op jit(solution)/shard_map/all_gather | solution.py:82
  187.5 4.1 %slice.83 = bf16[16,153600]{1,0:T(8,128)(2,1)} slice(bf16[16,204800]{1,0:T(8,128)(2,1)} %reshape.388), slice={[0:16], [0:153600]} | slice | bytes 9830400 | tf_op jit(solution)/shard_map/slice | solution.py:85
  191.6 12.3 %reshape.324 = bf16[16,3,640,80]{3,2,1,0:T(8,128)(2,1)} reshape(bf16[16,153600]{1,0:T(8,128)(2,1)} %slice.83) | data formatting | bytes 9830400 | tf_op jit(solution)/shard_map/reshape | solution.py:85
  203.9 9.6 %copy.78 = bf16[16,3,640,80]{2,3,1,0:T(8,128)(2,1)} copy(bf16[16,3,640,80]{3,2,1,0:T(8,128)(2,1)} %reshape.324) | data formatting | bytes 9830400 | tf_op jit(solution)/shard_map/optimization_barrier | solution.py:136
  214.9 4.9 %fusion.37 = f32[16,3,80,144]{2,3,1,0:T(8,128)S(1)} fusion(bf16[16,3,640,80]{3,2,1,0:T(8,128)(2,1)} %reshape.324, bf16[144,1280]{1,0:T(8,128)(2,1)S(1)} %reshape.326, s32[]{:T(128)S(6)} %select_n.65), kind=kOutput, calls=%fused_computation.53 | convolution fusion | flops 707788800 | bytes 7311364 | tf_op jit(solution)/shard_map/pc,jmcd->mpjd/dot_general | solution.py:142
  219.8 3.0 %collective-permute-done = bf16[16,3,640,80]{2,3,1,0:T(8,128)(2,1)} collective-permute-done((bf16[16,3,640,80]{2,3,1,0:T(8,128)(2,1)}, bf16[16,3,640,80]{2,3,1,0:T(8,128)(2,1)}, u32[]{:S(2)}, u32[]{:S(2)}) %collective-permute-start) | collective-permute-done | bytes 4915232 | tf_op jit(solution)/shard_map/ppermute | solution.py:138
  222.7 5.1 %fusion.13 = bf16[3,144,16,80]{3,1,0,2:T(8,128)(2,1)S(1)} fusion(f32[16,3,80,144]{2,3,1,0:T(8,128)S(1)} %fusion.37, bf16[16,3,640,80]{2,3,1,0:T(8,128)(2,1)} %collective-permute-done, bf16[144,1280]{1,0:T(8,128)(2,1)S(1)} %reshape.326, s32[]{:T(128)S(6)} %select_n.66), kind=kOutput, calls=%fused_computation.23 | convolution fusion | flops 708894720 | bytes 9744388 | tf_op jit(solution)/shard_map/pc,jmcd->mpjd/dot_general | solution.py:144
  228.1 2.2 reshape_squeeze.11
  230.5 2.2 reshape_squeeze.10
  232.8 1.3 reshape_squeeze.9
  234.1 3.2 %fusion.54 = (f32[9,20,16]{2,1,0:T(8,128)S(1)}, f32[9,20,16,16]{2,3,1,0:T(8,128)}) fusion(bf16[16,9,20,64]{3,2,1,0:T(8,128)(2,1)S(1)} %copy-done.4, bf16[16,9,20,64]{3,2,1,0:T(8,128)(2,1)} %reshape_squeeze.10, f32[20]{0:T(128)S(1)} %broadcast_multiply_fusion.1), kind=kOutput, calls=%fused_computation.77 | convolution fusion | flops 6036495 | bytes 933200 | tf_op jit(solution)/shard_map/sub | solution.py:28
  237.3 1.8 fusion.18
  239.9 10.0 %all_to_all.45 = bf16[8,2,1,9,1280]{4,0,3,2,1:T(8,128)(2,1)S(1)} all-to-all(bf16[8,2,1,9,1280]{4,0,3,2,1:T(8,128)(2,1)S(1)} %copy.87), channel_id=1, replica_groups=mesh['vz'=8,'vy'=2,'chip'=8,'core'=2] {'vy'}, dimensions={1} | all-to-all | bytes 737280 | tf_op jit(solution)/shard_map/all_to_all | solution.py:40
  250.9 4.2 %all-to-all-start.4 = ((bf16[8,2,1,9,1280]{4,1,3,2,0:T(2,128)(2,1)}), bf16[8,2,1,9,1280]{4,1,3,2,0:T(2,128)(2,1)S(1)}, u32[]{:S(2)}, u32[]{:S(2)}) async-start(bf16[8,2,1,9,1280]{4,1,3,2,0:T(2,128)(2,1)} %copy.88), calls=%async_computation.4 | async-start | bytes 737280 | tf_op jit(solution)/shard_map/all_to_all | solution.py:41
  255.1 1.7 reshape.323
  256.8 10.4 %all-to-all-done.4 = bf16[8,2,1,9,1280]{4,1,3,2,0:T(2,128)(2,1)S(1)} async-done(((bf16[8,2,1,9,1280]{4,1,3,2,0:T(2,128)(2,1)}), bf16[8,2,1,9,1280]{4,1,3,2,0:T(2,128)(2,1)S(1)}, u32[]{:S(2)}, u32[]{:S(2)}) %all-to-all-start.4) | async-done | bytes 368672 | tf_op jit(solution)/shard_map/all_to_all | solution.py:41
  267.6 3.1 %collective-permute-start.1 = (bf16[1280,640]{1,0:T(8,128)(2,1)}, bf16[1280,640]{1,0:T(8,128)(2,1)}, u32[]{:S(2)}, u32[]{:S(2)}) collective-permute-start(bf16[1280,640]{1,0:T(8,128)(2,1)} %reshape.323), channel_id=1, source_target_pairs={{0,1},{1,0},{2,3},{3,2},{4,5},{5,4},{6,7},{7,6},{8,9},{9,8},{10,11... | collective-permute-start | bytes 4915208 | tf_op jit(solution)/shard_map/ppermute | solution.py:150
  271.0 1.9 fusion.19
  274.2 1.9 fusion.22
  (79 shorter events, 17.2 us)
Async XLA Ops:
  6.5 50.5 %copy-start = (bf16[3,1280,80]{1,2,0:T(8,128)(2,1)S(1)}, bf16[3,1280,80]{1,2,0:T(8,128)(2,1)}, u32[]{:S(2)}) copy-start(bf16[3,1280,80]{1,2,0:T(8,128)(2,1)} %param.23) | copy-start | bytes 1843204
  6.5 54.6 %copy-start.2 = (bf16[3,3,1280,80]{2,3,1,0:T(8,128)(2,1)S(1)}, bf16[3,3,1280,80]{2,3,1,0:T(8,128)(2,1)}, u32[]{:S(2)}) copy-start(bf16[3,3,1280,80]{2,3,1,0:T(8,128)(2,1)} %param.20) | copy-start | bytes 5529604
  6.5 50.4 %all-gather.4.cloned.1.call-start = ((), (), s32[]{:S(2)}) async-start(), calls=%async_computation.5 | async-start | bytes 6266880 | tf_op jit(solution)/shard_map/all_gather | solution.py:74
  7.3 173.8 %all-gather.6.cloned.1.call-start = ((), (), s32[]{:S(2)}) async-start(), calls=%async_computation.6 | async-start | bytes 6963200 | tf_op jit(solution)/shard_map/all_gather | solution.py:82
  62.2 8.6 %copy-start.8 = (f32[1280]{0:T(1024)S(1)}, f32[1280]{0:T(1024)}, u32[]{:S(2)}) copy-start(f32[1280]{0:T(1024)} %param.15) | copy-start | bytes 15364
  62.2 8.6 %copy-start.9 = (f32[1280]{0:T(1024)S(1)}, f32[1280]{0:T(1024)}, u32[]{:S(2)}) copy-start(f32[1280]{0:T(1024)} %param.14) | copy-start | bytes 15364
  77.5 1.1 copy-start.5
  89.2 19.9 %copy-start.3 = (bf16[1,1,2,72,1280]{4,3,2,1,0:T(8,128)(2,1)S(1)}, bf16[1,1,2,72,1280]{4,3,2,1,0:T(8,128)(2,1)}, u32[]{:S(2)}) copy-start(bf16[1,1,2,72,1280]{4,3,2,1,0:T(8,128)(2,1)} %param.13) | copy-start | bytes 1105924
  89.2 19.9 %copy-start.6 = (f32[1280]{0:T(1024)S(1)}, f32[1280]{0:T(1024)}, u32[]{:S(2)}) copy-start(f32[1280]{0:T(1024)} %param.21) | copy-start | bytes 15364
  92.1 17.5 %copy-start.7 = (f32[1280]{0:T(1024)S(1)}, f32[1280]{0:T(1024)}, u32[]{:S(2)}) copy-start(f32[1280]{0:T(1024)} %param.22) | copy-start | bytes 15364
  203.9 10.7 %copy-start.10 = (f32[20]{0:T(128)S(1)}, f32[20]{0:T(128)}, u32[]{:S(2)}) copy-start(f32[20]{0:T(128)} %param.25) | copy-start | bytes 244
  213.5 9.3 %collective-permute-start = (bf16[16,3,640,80]{2,3,1,0:T(8,128)(2,1)}, bf16[16,3,640,80]{2,3,1,0:T(8,128)(2,1)}, u32[]{:S(2)}, u32[]{:S(2)}) collective-permute-start(bf16[16,3,640,80]{2,3,1,0:T(8,128)(2,1)} %copy.78), channel_id=1, source_target_pairs={{0,1},{1,0},{2,3},{3,2},{4,5},{5,4},{6,7},{7,6},{8,9},{9,8},{10,11... | collective-permute-start | bytes 14745608 | tf_op jit(solution)/shard_map/ppermute | solution.py:138
  230.3 3.8 %copy-start.4 = (bf16[16,9,20,64]{3,2,1,0:T(8,128)(2,1)S(1)}, bf16[16,9,20,64]{3,2,1,0:T(8,128)(2,1)}, u32[]{:S(2)}) copy-start(bf16[16,9,20,64]{3,2,1,0:T(8,128)(2,1)} %reshape_squeeze.11) | copy-start | bytes 1105924
  239.1 16.0 %slice-start = ((bf16[16,204800]{1,0:T(8,128)(2,1)}), bf16[16,51200]{1,0:T(8,128)(2,1)S(1)}, s32[]{:S(2)}) async-start(bf16[16,204800]{1,0:T(8,128)(2,1)} %reshape.388), calls=%async_computation.7 | async-start | bytes 3276800 | tf_op jit(solution)/shard_map/slice | solution.py:84
  250.9 16.3 %all-to-all-start.4 = ((bf16[8,2,1,9,1280]{4,1,3,2,0:T(2,128)(2,1)}), bf16[8,2,1,9,1280]{4,1,3,2,0:T(2,128)(2,1)S(1)}, u32[]{:S(2)}, u32[]{:S(2)}) async-start(bf16[8,2,1,9,1280]{4,1,3,2,0:T(2,128)(2,1)} %copy.88), calls=%async_computation.4 | async-start | bytes 737280 | tf_op jit(solution)/shard_map/all_to_all | solution.py:41
  255.1 21.9 %copy-start.1 = (bf16[3,1280,80]{1,2,0:T(8,128)(2,1)S(1)}, bf16[3,1280,80]{1,2,0:T(8,128)(2,1)}, u32[]{:S(2)}) copy-start(bf16[3,1280,80]{1,2,0:T(8,128)(2,1)} %param.23) | copy-start | bytes 1843204
  267.6 6.6 %collective-permute-start.1 = (bf16[1280,640]{1,0:T(8,128)(2,1)}, bf16[1280,640]{1,0:T(8,128)(2,1)}, u32[]{:S(2)}, u32[]{:S(2)}) collective-permute-start(bf16[1280,640]{1,0:T(8,128)(2,1)} %reshape.323), channel_id=1, source_target_pairs={{0,1},{1,0},{2,3},{3,2},{4,5},{5,4},{6,7},{7,6},{8,9},{9,8},{10,11... | collective-permute-start | bytes 4915208 | tf_op jit(solution)/shard_map/ppermute | solution.py:150
Sparse Core Ops, SparseCore 0:
  9.2 47.7 all-gather.3
  59.6 121.4 all-gather.5

commit v4 on v2

--- a/solution.py
+++ b/solution.py
@@ -34,12 +34,7 @@
 
 
 def send_back(mixed):
-    ys = lax.axis_size("vy")
-    zs = lax.axis_size("vz")
-    parts = mixed.reshape((zs, ys) + mixed.shape[1:])
-    parts = lax.all_to_all(parts, "vy", split_axis=1, concat_axis=1, tiled=True)
-    parts = lax.all_to_all(parts, "vz", split_axis=0, concat_axis=0, tiled=True)
-    return jnp.moveaxis(parts.reshape(mixed.shape), 0, 1)
+    return lax.all_to_all(mixed, VIEW, split_axis=0, concat_axis=1, tiled=True)
 
 
 def send_out(pixel_major):

time: 255 us -> 255 us (level)
    all_to_all x2 -> x1, blocking collectives: 26.3 us -> 25.6 us  [send_back(): return lax.all_to_all(mixed, VIEW, split_axis=0, concat_axis=1, tiled=True)]
where the time goes in v4:
time: 255 us
  blocking collectives  75.3 us (30%)
  waiting for transfers between devices  71.1 us (28%)
  local copies, waits for them, and re-layouts  30.9 us (12%)
  matrix products  23.2 us (9%)
  other arithmetic  22 us (9%)
  starting transfers between devices  17 us (7%)
  between operations  15.1 us (6%)
    all_gather x1, waiting for transfers between devices, local(): whole = lax.all_gather(latent, ROW, axis=2, tiled=True)  45.7 us
    all_to_all x1, blocking collectives, send_back(): return lax.all_to_all(mixed, VIEW, split_axis=0, concat_axis=1, tiled=True)  25.6 us
    all_gather x1, waiting for transfers between devices, local(): in_half = lax.all_gather(in_half, VIEW, axis=0, tiled=False)  20.3 us
    all_to_all x1, blocking collectives, send_out(): parts = lax.all_to_all(parts, 'vz', split_axis=1, concat_axis=1, tiled=True)  18.5 us
    all_to_all x1, blocking collectives, send_out(): parts = lax.all_to_all(parts, 'vy', split_axis=2, concat_axis=0, tiled=True)  15.8 us
    all_to_all x1, blocking collectives, local(): lax.all_to_all(conv_part, ROW, split_axis=2, concat_axis=4, tiled=True)  15.4 us
    all_to_all x1, starting transfers between devices, local(): lax.all_to_all(out_half, VIEW, split_axis=0, concat_axis=0, tiled=True)  11.7 us
    convert_element_type x1, other arithmetic, local(): activated = jax.nn.silu(hidden).astype(jnp.bfloat16)  8.52 us
  transfers between devices with their start and end apart: 5, of which 4 were waited for; matrix products, arithmetic and copies ran while one was open for 21% of the time, Pallas kernels for 0%

profile of v4, /device:TPU:1, one launch (start us, length us, event | category | flops | bytes accessed | tf_op | source)
XLA Modules:
  0.0 254.6 jit_solution(9439201119300199080)
XLA Ops:
  8.2 1.3 broadcast_in_dim.26
  9.5 11.7 %all-to-all-start = ((bf16[16,80,640]{2,1,0:T(8,128)(2,1)}), bf16[16,80,640]{2,1,0:T(8,128)(2,1)S(1)}, u32[]{:S(2)}, u32[]{:S(2)}) async-start(bf16[16,80,640]{2,1,0:T(8,128)(2,1)} %broadcast_in_dim.26), calls=%async_computation | async-start | bytes 3276800 | tf_op jit(solution)/shard_map/all_to_all | solution.py:79
  23.5 2.6 %fusion.52 = (bf16[1,3,1280,80]{2,3,1,0:T(8,128)(2,1)S(1)}, bf16[1,3,1280,80]{2,3,1,0:T(8,128)(2,1)}, bf16[1,3,1280,80]{2,3,1,0:T(8,128)(2,1)}) fusion(bf16[3,3,1280,80]{2,3,1,0:T(8,128)(2,1)} %param.20), kind=kLoop, calls=%fused_computation.74 | loop fusion | bytes 3686400 | tf_op jit(solution)/shard_map/slice | solution.py:104
  26.1 45.7 %all-gather.4.cloned.1.call-done = bf16[1,1,32,72,1280]{4,3,1,0,2:T(8,128)(2,1)} async-done(((bf16[1,1,2,72,1280]{4,3,1,0,2:T(8,128)(2,1)}), bf16[1,1,32,72,1280]{4,3,1,0,2:T(8,128)(2,1)}) %all-gather.4.cloned.1.call-update) | async-done | bytes 5898256 | tf_op jit(solution)/shard_map/all_gather | solution.py:69
  71.9 3.5 %convert_reduce_fusion = f32[1280]{0:T(1024)S(1)} fusion(bf16[1,1,32,72,1280]{4,3,1,0,2:T(8,128)(2,1)} %all-gather.4.cloned.1.call-done), kind=kLoop, calls=%fused_computation.2 | loop fusion | flops 5896960 | bytes 5903360 | tf_op jit(solution)/shard_map/reduce_sum | solution.py:87
  76.6 4.3 %fusion.3 = f32[1280]{0:T(1024)S(1)} fusion(bf16[1,1,32,72,1280]{4,3,1,0,2:T(8,128)(2,1)} %all-gather.4.cloned.1.call-done, f32[1280]{0:T(1024)S(1)} %sub.42), kind=kLoop, calls=%fused_computation.5 | loop fusion | flops 11795200 | bytes 5908480 | tf_op jit(solution)/shard_map/reduce_sum | solution.py:89
  81.2 8.5 %multiply_convert_fusion = bf16[1,1,32,72,1280]{4,3,1,0,2:T(8,128)(2,1)} fusion(bf16[1,1,32,72,1280]{4,3,1,0,2:T(8,128)(2,1)} %all-gather.4.cloned.1.call-done, f32[1280]{0:T(1024)S(1)} %get-tuple-element.44, f32[1280]{0:T(1024)S(1)} %get-tuple-element.43, f32[1280]{0:T(1024)S(1)} %copy-done.11, f32[1280]{0:T(1024)S(1)} %copy-done.12, f32[1280]{0:T(1024)S(1)} %mul.83, ...), kind=kLoop, calls=%fused_computation.10 | loop fusion | flops 35389440 | bytes 11827200 | tf_op jit(solution)/shard_map/convert_element_type | solution.py:97
  89.8 5.6 %pad_slice_fusion = (bf16[1,1,32,72,1280]{4,3,1,0,2:T(8,128)(2,1)S(1)}, bf16[1,1,32,72,1280]{4,3,1,0,2:T(8,128)(2,1)S(1)}) fusion(bf16[1,1,32,72,1280]{4,3,1,0,2:T(8,128)(2,1)} %multiply_convert_fusion), kind=kLoop, calls=%fused_computation.11 | loop fusion | bytes 17694720 | tf_op jit(solution)/shard_map/slice | solution.py:103
  95.4 1.7 fusion.59
  98.2 1.8 convolution_add_fusion.1
  100.0 1.8 convolution_add_fusion
  101.8 5.2 %reshape.319 = f32[1,1,32,72,3,80]{3,2,5,4,1,0:T(8,128)} reshape(f32[2304,240]{0,1:T(8,128)S(1)} %convolution_add_fusion) | data formatting | bytes 4423680 | tf_op jit(solution)/shard_map/reshape | solution.py:107
  107.1 2.9 %fusion.35 = bf16[1,1,32,72,80]{3,2,4,1,0:T(8,128)(2,1)S(1)} fusion(f32[1,1,32,72,3,80]{3,2,5,4,1,0:T(8,128)} %reshape.319), kind=kLoop, calls=%fused_computation.50 | loop fusion | flops 552960 | bytes 5611520 | tf_op jit(solution)/shard_map/convert_element_type | solution.py:115
  110.7 15.4 %all_to_all.49 = bf16[1,1,32,72,80]{4,3,1,0,2:T(8,128)(2,1)S(1)} all-to-all(bf16[1,1,32,72,80]{4,3,1,0,2:T(8,128)(2,1)S(1)} %copy.57), channel_id=1, replica_groups=mesh['vz'=8,'vy'=2,'chip'=8,'core'=2] {'chip','core'}, dimensions={2} | all-to-all | bytes 737280 | tf_op jit(solution)/shard_map/all_to_all | solution.py:116
  128.1 15.8 %all_to_all.50 = bf16[1,8,2,9,1280]{4,1,3,0,2:T(8,128)(2,1)S(1)} all-to-all(bf16[1,8,2,9,1280]{4,1,3,0,2:T(8,128)(2,1)S(1)} %copy.59), channel_id=1, replica_groups=mesh['vz'=8,'vy'=2,'chip'=8,'core'=2] {'vy'}, dimensions={2} | all-to-all | bytes 737280 | tf_op jit(solution)/shard_map/all_to_all | solution.py:45
  144.1 18.5 %all_to_all.51 = bf16[2,8,1,9,1280]{4,0,3,2,1:T(2,128)(2,1)S(1)} all-to-all(bf16[2,8,1,9,1280]{4,0,3,2,1:T(2,128)(2,1)S(1)} %copy.60), channel_id=1, replica_groups=mesh['vz'=8,'vy'=2,'chip'=8,'core'=2] {'vz'}, dimensions={1} | all-to-all | bytes 737280 | tf_op jit(solution)/shard_map/all_to_all | solution.py:46
  163.0 20.3 %all-gather.6.cloned.1.call-done = bf16[48,640,80]{1,2,0:T(8,128)(2,1)} async-done(((bf16[3,640,80]{1,2,0:T(8,128)(2,1)}), bf16[48,640,80]{1,2,0:T(8,128)(2,1)}) %all-gather.6.cloned.1.call-update) | async-done | bytes 4915216 | tf_op jit(solution)/shard_map/all_gather | solution.py:75
  183.4 3.2 %collective-permute-start = (bf16[16,3,640,80]{2,3,1,0:T(8,128)(2,1)}, bf16[16,3,640,80]{2,3,1,0:T(8,128)(2,1)}, u32[]{:S(2)}, u32[]{:S(2)}) collective-permute-start(bf16[16,3,640,80]{2,3,1,0:T(8,128)(2,1)} %bitcast.97), channel_id=1, source_target_pairs={{0,1},{1,0},{2,3},{3,2},{4,5},{5,4},{6,7},{7,6},{8,9},{9,8},{10,11... | collective-permute-start | bytes 14745608 | tf_op jit(solution)/shard_map/ppermute | solution.py:134
  186.9 5.1 %fusion.37 = f32[16,3,80,144]{2,3,1,0:T(8,128)S(1)} fusion(bf16[16,3,640,80]{2,3,1,0:T(8,128)(2,1)} %bitcast.98, bf16[144,1280]{1,0:T(8,128)(2,1)S(1)} %reshape.321, s32[]{:T(128)S(6)} %select_n.60), kind=kOutput, calls=%fused_computation.52 | convolution fusion | flops 707788800 | bytes 7311364 | tf_op jit(solution)/shard_map/pc,jmcd->mpjd/dot_general | solution.py:138
  192.0 2.8 %collective-permute-done = bf16[16,3,640,80]{2,3,1,0:T(8,128)(2,1)} collective-permute-done((bf16[16,3,640,80]{2,3,1,0:T(8,128)(2,1)}, bf16[16,3,640,80]{2,3,1,0:T(8,128)(2,1)}, u32[]{:S(2)}, u32[]{:S(2)}) %collective-permute-start) | collective-permute-done | bytes 4915232 | tf_op jit(solution)/shard_map/ppermute | solution.py:134
  194.7 5.1 %fusion.13 = bf16[3,144,16,80]{3,1,0,2:T(8,128)(2,1)S(1)} fusion(f32[16,3,80,144]{2,3,1,0:T(8,128)S(1)} %fusion.37, bf16[16,3,640,80]{2,3,1,0:T(8,128)(2,1)} %collective-permute-done, bf16[144,1280]{1,0:T(8,128)(2,1)S(1)} %reshape.321, s32[]{:T(128)S(6)} %select_n.66), kind=kOutput, calls=%fused_computation.23 | convolution fusion | flops 708894720 | bytes 9744388 | tf_op jit(solution)/shard_map/pc,jmcd->mpjd/dot_general | solution.py:140
  200.1 2.2 reshape_squeeze.10
  202.5 2.2 reshape_squeeze.11
  204.9 2.2 reshape_squeeze.9
  207.1 3.2 %fusion.54 = (f32[9,20,16]{2,1,0:T(8,128)S(1)}, f32[9,20,16,16]{2,3,1,0:T(8,128)}) fusion(bf16[16,9,20,64]{3,2,1,0:T(8,128)(2,1)} %reshape_squeeze.11, bf16[16,9,20,64]{3,2,1,0:T(8,128)(2,1)S(1)} %copy-done.7, f32[20]{0:T(128)S(1)} %broadcast_multiply_fusion.1), kind=kOutput, calls=%fused_computation.76 | convolution fusion | flops 6036495 | bytes 933200 | tf_op jit(solution)/shard_map/sub | solution.py:28
  210.3 2.2 fusion.18
  212.7 1.5 reshape.389
  214.2 25.6 %all_to_all.52 = bf16[16,1,9,1280]{3,2,1,0:T(8,128)(2,1)} all-to-all(bf16[16,1,9,1280]{3,2,1,0:T(8,128)(2,1)} %reshape.389), channel_id=1, replica_groups=mesh['vz'=8,'vy'=2,'chip'=8,'core'=2] {'vz','vy'}, dimensions={0} | all-to-all | bytes 737280 | tf_op jit(solution)/shard_map/all_to_all | solution.py:37
  239.7 2.0 collective-permute-start.1
  241.7 1.3 reshape.323
  243.5 1.5 collective-permute-done.1
  245.0 1.9 fusion.22
  (70 shorter events, 10.8 us)
Async XLA Ops:
  6.5 69.0 %copy-start = (bf16[3,1280,80]{1,2,0:T(8,128)(2,1)S(1)}, bf16[3,1280,80]{1,2,0:T(8,128)(2,1)}, u32[]{:S(2)}) copy-start(bf16[3,1280,80]{1,2,0:T(8,128)(2,1)} %param.23) | copy-start | bytes 1843204
  6.5 65.3 %all-gather.4.cloned.1.call-start = ((), (), s32[]{:S(2)}) async-start(), calls=%async_computation.5 | async-start | bytes 6266880 | tf_op jit(solution)/shard_map/all_gather | solution.py:69
  9.5 80.3 %all-to-all-start = ((bf16[16,80,640]{2,1,0:T(8,128)(2,1)}), bf16[16,80,640]{2,1,0:T(8,128)(2,1)S(1)}, u32[]{:S(2)}, u32[]{:S(2)}) async-start(bf16[16,80,640]{2,1,0:T(8,128)(2,1)} %broadcast_in_dim.26), calls=%async_computation | async-start | bytes 3276800 | tf_op jit(solution)/shard_map/all_to_all | solution.py:79
  21.3 162.1 %all-gather.6.cloned.1.call-start = ((), (), s32[]{:S(2)}) async-start(), calls=%async_computation.6 | async-start | bytes 5222400 | tf_op jit(solution)/shard_map/all_gather | solution.py:75
  75.4 5.8 %copy-start.11 = (f32[1280]{0:T(1024)S(1)}, f32[1280]{0:T(1024)}, u32[]{:S(2)}) copy-start(f32[1280]{0:T(1024)} %param.15) | copy-start | bytes 15364
  75.4 5.8 %copy-start.12 = (f32[1280]{0:T(1024)S(1)}, f32[1280]{0:T(1024)}, u32[]{:S(2)}) copy-start(f32[1280]{0:T(1024)} %param.14) | copy-start | bytes 15364
  89.8 5.6 %copy-start.3 = (bf16[16,80,640]{2,1,0:T(8,128)(2,1)}, bf16[16,80,640]{2,1,0:T(8,128)(2,1)S(1)}, u32[]{:S(2)}) copy-start(bf16[16,80,640]{2,1,0:T(8,128)(2,1)S(1)} %all-to-all-done) | copy-start | bytes 4915204
  89.8 5.6 %copy-start.8 = (bf16[1,3,1280,80]{2,3,1,0:T(8,128)(2,1)S(1)}, bf16[1,3,1280,80]{2,3,1,0:T(8,128)(2,1)}, u32[]{:S(2)}) copy-start(bf16[1,3,1280,80]{2,3,1,0:T(8,128)(2,1)} %get-tuple-element.50) | copy-start | bytes 1843204
  95.4 2.7 %copy-start.2 = (bf16[1,1,32,72,1280]{4,3,1,0,2:T(8,128)(2,1)S(1)}, bf16[1,1,32,72,1280]{4,3,1,0,2:T(8,128)(2,1)}, u32[]{:S(2)}) copy-start(bf16[1,1,32,72,1280]{4,3,1,0,2:T(8,128)(2,1)} %multiply_convert_fusion) | copy-start | bytes 17694724
  95.4 2.8 %copy-start.5 = (bf16[1,3,1280,80]{2,3,1,0:T(8,128)(2,1)S(1)}, bf16[1,3,1280,80]{2,3,1,0:T(8,128)(2,1)}, u32[]{:S(2)}) copy-start(bf16[1,3,1280,80]{2,3,1,0:T(8,128)(2,1)} %get-tuple-element.51) | copy-start | bytes 1843204
  107.1 19.8 %copy-start.6 = (bf16[1,1,2,72,1280]{4,3,2,1,0:T(8,128)(2,1)S(1)}, bf16[1,1,2,72,1280]{4,3,2,1,0:T(8,128)(2,1)}, u32[]{:S(2)}) copy-start(bf16[1,1,2,72,1280]{4,3,2,1,0:T(8,128)(2,1)} %param.13) | copy-start | bytes 1105924
  107.1 19.8 %copy-start.9 = (f32[1280]{0:T(1024)S(1)}, f32[1280]{0:T(1024)}, u32[]{:S(2)}) copy-start(f32[1280]{0:T(1024)} %param.21) | copy-start | bytes 15364
  110.0 17.4 %copy-start.10 = (f32[1280]{0:T(1024)S(1)}, f32[1280]{0:T(1024)}, u32[]{:S(2)}) copy-start(f32[1280]{0:T(1024)} %param.22) | copy-start | bytes 15364
  126.3 60.3 %copy-start.13 = (f32[20]{0:T(128)S(1)}, f32[20]{0:T(128)}, u32[]{:S(2)}) copy-start(f32[20]{0:T(128)} %param.25) | copy-start | bytes 244
  183.4 11.4 %collective-permute-start = (bf16[16,3,640,80]{2,3,1,0:T(8,128)(2,1)}, bf16[16,3,640,80]{2,3,1,0:T(8,128)(2,1)}, u32[]{:S(2)}, u32[]{:S(2)}) collective-permute-start(bf16[16,3,640,80]{2,3,1,0:T(8,128)(2,1)} %bitcast.97), channel_id=1, source_target_pairs={{0,1},{1,0},{2,3},{3,2},{4,5},{5,4},{6,7},{7,6},{8,9},{9,8},{10,11... | collective-permute-start | bytes 14745608 | tf_op jit(solution)/shard_map/ppermute | solution.py:134
  202.3 4.7 %copy-start.7 = (bf16[16,9,20,64]{3,2,1,0:T(8,128)(2,1)S(1)}, bf16[16,9,20,64]{3,2,1,0:T(8,128)(2,1)}, u32[]{:S(2)}) copy-start(bf16[16,9,20,64]{3,2,1,0:T(8,128)(2,1)} %reshape_squeeze.10) | copy-start | bytes 1105924
  210.3 29.5 %copy-start.4 = (bf16[16,80,640]{2,1,0:T(8,128)(2,1)S(1)}, bf16[16,80,640]{2,1,0:T(8,128)(2,1)}, u32[]{:S(2)}) copy-start(bf16[16,80,640]{2,1,0:T(8,128)(2,1)} %copy-done.3) | copy-start | bytes 4915204
  212.4 35.3 %copy-start.1 = (bf16[3,1280,80]{1,2,0:T(8,128)(2,1)S(1)}, bf16[3,1280,80]{1,2,0:T(8,128)(2,1)}, u32[]{:S(2)}) copy-start(bf16[3,1280,80]{1,2,0:T(8,128)(2,1)} %param.23) | copy-start | bytes 1843204
  239.7 5.3 %collective-permute-start.1 = (bf16[1280,640]{1,0:T(8,128)(2,1)S(1)}, bf16[1280,640]{1,0:T(8,128)(2,1)}, u32[]{:S(2)}, u32[]{:S(2)}) collective-permute-start(bf16[1280,640]{1,0:T(8,128)(2,1)S(1)} %bitcast.99), channel_id=1, source_target_pairs={{0,1},{1,0},{2,3},{3,2},{4,5},{5,4},{6,7},{7,6},{8,9},{9,8},{10,11... | collective-permute-start | bytes 4915208 | tf_op jit(solution)/shard_map/ppermute | solution.py:146
Sparse Core Ops, SparseCore 0:
  9.2 62.6 all-gather.3
  76.4 106.9 all-gather.5

commit v5 on v4

--- a/solution.py
+++ b/solution.py
@@ -96,6 +96,8 @@
     hidden = (normed * gn_gain + gn_bias) * (1.0 + film_scale) + film_shift
     activated = jax.nn.silu(hidden).astype(jnp.bfloat16)
     out_half, activated = lax.optimization_barrier((out_half, activated))
+    swap = [(0, 1), (1, 0)]
+    out_other = lax.ppermute(out_half, "core", swap)
     taps = conv_w.shape[1]
     padded = jnp.pad(activated, ((0, 0), (0, 0), (1, 1), (0, 0), (0, 0)))
     tap_sum = None
@@ -114,6 +116,7 @@
     me = lax.axis_index("chip") * lax.axis_size("core") + core
     conv_part = conv_out.astype(jnp.bfloat16)
     conv_rows = lax.all_to_all(conv_part, ROW, split_axis=2, concat_axis=4, tiled=True)
+    out_other, conv_rows = lax.optimization_barrier((out_other, conv_rows))
     resid_out = (
         latent.astype(jnp.float32) + conv_rows.astype(jnp.float32) + conv_bias
     ).astype(jnp.bfloat16)
@@ -130,7 +133,6 @@
     )
     views = send_out(pixel_major)
     in_half, views = lax.optimization_barrier((in_half, views))
-    swap = [(0, 1), (1, 0)]
     in_other = lax.ppermute(in_half, "core", swap)
     flat_block = views.reshape(-1, width_out)
     block_mine = lax.dynamic_slice_in_dim(flat_block, core * half_in, half_in, axis=1)
@@ -142,8 +144,6 @@
     )
     triple_in = triple_in.astype(jnp.bfloat16).reshape((3,) + views.shape)
     mixed = send_back(attend(triple_in[0], triple_in[1], triple_in[2], head_scale))
-    out_half, mixed = lax.optimization_barrier((out_half, mixed))
-    out_other = lax.ppermute(out_half, "core", swap)
     mixed = jnp.moveaxis(
         mixed.reshape(local_views, samples, local_rows, local_cols, width_out), 0, 1
     )

time: 255 us -> 251 us (0.984)
  blocking collectives: 75.3 us -> 50.2 us
  waiting for transfers between devices: 71.1 us -> 90.6 us
  local copies, waits for them, and re-layouts: 30.9 us -> 27.1 us
  starting transfers between devices: 17 us -> 19.7 us
    all_to_all x1 -> x0, blocking collectives: 25.6 us -> none  [send_back(): return lax.all_to_all(mixed, VIEW, split_axis=0, concat_axis=1, tiled=True)]
    all_to_all x0 -> x1, waiting for transfers between devices: none -> 20 us  [send_back(): return lax.all_to_all(mixed, VIEW, split_axis=0, concat_axis=1, tiled=True)]
    all_to_all x0 -> x1, starting transfers between devices: none -> 4.29 us  [send_back(): return lax.all_to_all(mixed, VIEW, split_axis=0, concat_axis=1, tiled=True)]
  transfers between devices with their start and end apart: 5 -> 6, of which waited for: 4 -> 4; matrix products, arithmetic and copies ran while one was open for 21% -> 20% of each run, Pallas kernels for 0% -> 0%
where the time goes in v5:
time: 251 us; the launch traced here: 249 us
  waiting for transfers between devices  90.6 us (36%)
  blocking collectives  50.2 us (20%)
  local copies, waits for them, and re-layouts  27.1 us (11%)
  matrix products  24.5 us (10%)
  other arithmetic  21.8 us (9%)
  starting transfers between devices  19.7 us (8%)
  between operations  15.1 us (6%)
    all_gather x1, waiting for transfers between devices, local(): whole = lax.all_gather(latent, ROW, axis=2, tiled=True)  46.8 us
    all_gather x1, waiting for transfers between devices, local(): in_half = lax.all_gather(in_half, VIEW, axis=0, tiled=False)  20.4 us
    all_to_all x1, waiting for transfers between devices, send_back(): return lax.all_to_all(mixed, VIEW, split_axis=0, concat_axis=1, tiled=True)  20 us
    all_to_all x1, blocking collectives, send_out(): parts = lax.all_to_all(parts, 'vz', split_axis=1, concat_axis=1, tiled=True)  19.1 us
    all_to_all x1, blocking collectives, send_out(): parts = lax.all_to_all(parts, 'vy', split_axis=2, concat_axis=0, tiled=True)  15.8 us
    all_to_all x1, blocking collectives, local(): lax.all_to_all(conv_part, ROW, split_axis=2, concat_axis=4, tiled=True)  15.4 us
    all_to_all x1, starting transfers between devices, local(): lax.all_to_all(out_half, VIEW, split_axis=0, concat_axis=0, tiled=True)  11.8 us
    convert_element_type x1, other arithmetic, local(): activated = jax.nn.silu(hidden).astype(jnp.bfloat16)  8.36 us
  transfers between devices with their start and end apart: 6, of which 4 were waited for; matrix products, arithmetic and copies ran while one was open for 20% of the time, Pallas kernels for 0%

profile of v5, /device:TPU:1, one launch (start us, length us, event | category | flops | bytes accessed | tf_op | source)
XLA Modules:
  0.0 249.1 jit_solution(865494250867244917)
XLA Ops:
  8.2 1.3 broadcast_in_dim.26
  9.5 11.8 %all-to-all-start = ((bf16[16,80,640]{2,1,0:T(8,128)(2,1)}), bf16[16,80,640]{2,1,0:T(8,128)(2,1)}, u32[]{:S(2)}, u32[]{:S(2)}) async-start(bf16[16,80,640]{2,1,0:T(8,128)(2,1)} %broadcast_in_dim.26), calls=%async_computation | async-start | bytes 3276800 | tf_op jit(solution)/shard_map/all_to_all | solution.py:79
  23.5 1.6 fusion.52
  25.1 46.8 %all-gather.4.cloned.1.call-done = bf16[1,1,32,72,1280]{4,3,1,0,2:T(8,128)(2,1)} async-done(((bf16[1,1,2,72,1280]{4,3,1,0,2:T(8,128)(2,1)}), bf16[1,1,32,72,1280]{4,3,1,0,2:T(8,128)(2,1)}) %all-gather.4.cloned.1.call-update) | async-done | bytes 5898256 | tf_op jit(solution)/shard_map/all_gather | solution.py:69
  71.9 3.5 %convert_reduce_fusion = f32[1280]{0:T(1024)S(1)} fusion(bf16[1,1,32,72,1280]{4,3,1,0,2:T(8,128)(2,1)} %all-gather.4.cloned.1.call-done), kind=kLoop, calls=%fused_computation.2 | loop fusion | flops 5896960 | bytes 5903360 | tf_op jit(solution)/shard_map/reduce_sum | solution.py:87
  76.6 4.3 %fusion.3 = f32[1280]{0:T(1024)S(1)} fusion(bf16[1,1,32,72,1280]{4,3,1,0,2:T(8,128)(2,1)} %all-gather.4.cloned.1.call-done, f32[1280]{0:T(1024)S(1)} %sub.42), kind=kLoop, calls=%fused_computation.5 | loop fusion | flops 11795200 | bytes 5908480 | tf_op jit(solution)/shard_map/reduce_sum | solution.py:89
  81.2 8.4 %multiply_convert_fusion = bf16[1,1,32,72,1280]{4,3,1,0,2:T(8,128)(2,1)} fusion(bf16[1,1,32,72,1280]{4,3,1,0,2:T(8,128)(2,1)} %all-gather.4.cloned.1.call-done, f32[1280]{0:T(1024)S(1)} %get-tuple-element.44, f32[1280]{0:T(1024)S(1)} %get-tuple-element.43, f32[1280]{0:T(1024)S(1)} %copy-done.6, f32[1280]{0:T(1024)S(1)} %copy-done.7, f32[1280]{0:T(1024)S(1)} %mul.83, ...), kind=kLoop, calls=%fused_computation.10 | loop fusion | flops 35389440 | bytes 11827200 | tf_op jit(solution)/shard_map/convert_element_type | solution.py:97
  89.9 5.0 %pad_slice_fusion = (bf16[1,1,32,72,1280]{4,3,1,0,2:T(8,128)(2,1)S(1)}, bf16[1,1,32,72,1280]{4,3,1,0,2:T(8,128)(2,1)S(1)}) fusion(bf16[1,1,32,72,1280]{4,3,1,0,2:T(8,128)(2,1)} %multiply_convert_fusion), kind=kLoop, calls=%fused_computation.11 | loop fusion | bytes 17694720 | tf_op jit(solution)/shard_map/slice | solution.py:105
  94.9 1.7 fusion.59
  96.6 1.0 copy-done.2
  97.6 1.8 convolution_add_fusion.1
  99.4 1.8 convolution_add_fusion
  101.2 5.2 %reshape.304 = f32[1,1,32,72,3,80]{3,2,5,4,1,0:T(8,128)} reshape(f32[2304,240]{0,1:T(8,128)S(1)} %convolution_add_fusion) | data formatting | bytes 4423680 | tf_op jit(solution)/shard_map/reshape | solution.py:109
  106.4 2.9 %fusion.35 = bf16[1,1,32,72,80]{3,2,4,1,0:T(8,128)(2,1)S(1)} fusion(f32[1,1,32,72,3,80]{3,2,5,4,1,0:T(8,128)} %reshape.304), kind=kLoop, calls=%fused_computation.49 | loop fusion | flops 552960 | bytes 5611520 | tf_op jit(solution)/shard_map/convert_element_type | solution.py:117
  110.1 15.4 %all_to_all.55 = bf16[1,1,32,72,80]{4,3,1,0,2:T(8,128)(2,1)S(1)} all-to-all(bf16[1,1,32,72,80]{4,3,1,0,2:T(8,128)(2,1)S(1)} %copy.57), channel_id=1, replica_groups=mesh['vz'=8,'vy'=2,'chip'=8,'core'=2] {'chip','core'}, dimensions={2} | all-to-all | bytes 737280 | tf_op jit(solution)/shard_map/all_to_all | solution.py:118
  127.4 15.8 %all_to_all.56 = bf16[1,8,2,9,1280]{4,1,3,0,2:T(8,128)(2,1)S(1)} all-to-all(bf16[1,8,2,9,1280]{4,1,3,0,2:T(8,128)(2,1)S(1)} %copy.59), channel_id=1, replica_groups=mesh['vz'=8,'vy'=2,'chip'=8,'core'=2] {'vy'}, dimensions={2} | all-to-all | bytes 737280 | tf_op jit(solution)/shard_map/all_to_all | solution.py:45
  143.5 19.1 %all_to_all.57 = bf16[2,8,1,9,1280]{4,0,3,2,1:T(2,128)(2,1)S(1)} all-to-all(bf16[2,8,1,9,1280]{4,0,3,2,1:T(2,128)(2,1)S(1)} %copy.60), channel_id=1, replica_groups=mesh['vz'=8,'vy'=2,'chip'=8,'core'=2] {'vz'}, dimensions={1} | all-to-all | bytes 737280 | tf_op jit(solution)/shard_map/all_to_all | solution.py:46
  163.0 20.4 %all-gather.6.cloned.1.call-done = bf16[48,640,80]{1,2,0:T(8,128)(2,1)} async-done(((bf16[3,640,80]{1,2,0:T(8,128)(2,1)}), bf16[48,640,80]{1,2,0:T(8,128)(2,1)}) %all-gather.6.cloned.1.call-update) | async-done | bytes 4915216 | tf_op jit(solution)/shard_map/all_gather | solution.py:75
  183.3 3.3 %collective-permute-start.1 = (bf16[16,3,640,80]{2,3,1,0:T(8,128)(2,1)}, bf16[16,3,640,80]{2,3,1,0:T(8,128)(2,1)}, u32[]{:S(2)}, u32[]{:S(2)}) collective-permute-start(bf16[16,3,640,80]{2,3,1,0:T(8,128)(2,1)} %bitcast.95), channel_id=1, source_target_pairs={{0,1},{1,0},{2,3},{3,2},{4,5},{5,4},{6,7},{7,6},{8,9},{9,8},{10,11... | collective-permute-start | bytes 14745608 | tf_op jit(solution)/shard_map/ppermute | solution.py:136
  187.0 5.1 %fusion.37 = f32[16,3,80,144]{2,3,1,0:T(8,128)S(1)} fusion(bf16[16,3,640,80]{2,3,1,0:T(8,128)(2,1)} %bitcast.96, bf16[144,1280]{1,0:T(8,128)(2,1)S(1)} %reshape.306, s32[]{:T(128)S(6)} %select_n.60), kind=kOutput, calls=%fused_computation.52 | convolution fusion | flops 707788800 | bytes 7311364 | tf_op jit(solution)/shard_map/pc,jmcd->mpjd/dot_general | solution.py:140
  192.0 2.8 %collective-permute-done.1 = bf16[16,3,640,80]{2,3,1,0:T(8,128)(2,1)} collective-permute-done((bf16[16,3,640,80]{2,3,1,0:T(8,128)(2,1)}, bf16[16,3,640,80]{2,3,1,0:T(8,128)(2,1)}, u32[]{:S(2)}, u32[]{:S(2)}) %collective-permute-start.1) | collective-permute-done | bytes 4915232 | tf_op jit(solution)/shard_map/ppermute | solution.py:136
  194.8 5.1 %fusion.13 = bf16[3,144,16,80]{3,1,0,2:T(8,128)(2,1)S(1)} fusion(f32[16,3,80,144]{2,3,1,0:T(8,128)S(1)} %fusion.37, bf16[16,3,640,80]{2,3,1,0:T(8,128)(2,1)} %collective-permute-done.1, bf16[144,1280]{1,0:T(8,128)(2,1)S(1)} %reshape.306, s32[]{:T(128)S(6)} %select_n.66), kind=kOutput, calls=%fused_computation.23 | convolution fusion | flops 708894720 | bytes 9744388 | tf_op jit(solution)/shard_map/pc,jmcd->mpjd/dot_general | solution.py:142
  200.2 1.3 reshape_squeeze.10
  201.6 2.2 reshape_squeeze.11
  204.0 2.2 reshape_squeeze.9
  206.1 3.2 %fusion.54 = (f32[9,20,16]{2,1,0:T(8,128)S(1)}, f32[9,20,16,16]{2,3,1,0:T(8,128)}) fusion(bf16[16,9,20,64]{3,2,1,0:T(8,128)(2,1)} %reshape_squeeze.11, bf16[16,9,20,64]{3,2,1,0:T(8,128)(2,1)S(1)} %reshape_squeeze.10, f32[20]{0:T(128)S(1)} %broadcast_multiply_fusion.1), kind=kOutput, calls=%fused_computation.76 | convolution fusion | flops 6036495 | bytes 933200 | tf_op jit(solution)/shard_map/sub | solution.py:28
  209.3 2.1 fusion.18
  211.6 1.5 reshape.372
  213.1 4.3 %all-to-all-start.4 = ((bf16[16,1,9,1280]{3,2,1,0:T(8,128)(2,1)}), bf16[16,1,9,1280]{3,2,1,0:T(8,128)(2,1)S(1)}, u32[]{:S(2)}, u32[]{:S(2)}) async-start(bf16[16,1,9,1280]{3,2,1,0:T(8,128)(2,1)} %reshape.372), calls=%async_computation.4 | async-start | bytes 1310720 | tf_op jit(solution)/shard_map/all_to_all | solution.py:37
  217.4 20.0 %all-to-all-done.4 = bf16[16,1,9,1280]{3,2,1,0:T(8,128)(2,1)S(1)} async-done(((bf16[16,1,9,1280]{3,2,1,0:T(8,128)(2,1)}), bf16[16,1,9,1280]{3,2,1,0:T(8,128)(2,1)S(1)}, u32[]{:S(2)}, u32[]{:S(2)}) %all-to-all-start.4) | async-done | bytes 368672 | tf_op jit(solution)/shard_map/all_to_all | solution.py:37
  237.5 1.9 fusion.19
  239.4 1.9 fusion.22
  (61 shorter events, 9.8 us)
Async XLA Ops:
  6.5 69.0 %copy-start = (bf16[3,1280,80]{1,2,0:T(8,128)(2,1)S(1)}, bf16[3,1280,80]{1,2,0:T(8,128)(2,1)}, u32[]{:S(2)}) copy-start(bf16[3,1280,80]{1,2,0:T(8,128)(2,1)} %param.23) | copy-start | bytes 1843204
  6.5 65.3 %all-gather.4.cloned.1.call-start = ((), (), s32[]{:S(2)}) async-start(), calls=%async_computation.5 | async-start | bytes 6266880 | tf_op jit(solution)/shard_map/all_gather | solution.py:69
  9.5 80.1 %all-to-all-start = ((bf16[16,80,640]{2,1,0:T(8,128)(2,1)}), bf16[16,80,640]{2,1,0:T(8,128)(2,1)}, u32[]{:S(2)}, u32[]{:S(2)}) async-start(bf16[16,80,640]{2,1,0:T(8,128)(2,1)} %broadcast_in_dim.26), calls=%async_computation | async-start | bytes 3276800 | tf_op jit(solution)/shard_map/all_to_all | solution.py:79
  21.3 162.1 %all-gather.6.cloned.1.call-start = ((), (), s32[]{:S(2)}) async-start(), calls=%async_computation.6 | async-start | bytes 5222400 | tf_op jit(solution)/shard_map/all_gather | solution.py:75
  75.4 5.8 %copy-start.6 = (f32[1280]{0:T(1024)S(1)}, f32[1280]{0:T(1024)}, u32[]{:S(2)}) copy-start(f32[1280]{0:T(1024)} %param.15) | copy-start | bytes 15364
  75.4 5.8 %copy-start.7 = (f32[1280]{0:T(1024)S(1)}, f32[1280]{0:T(1024)}, u32[]{:S(2)}) copy-start(f32[1280]{0:T(1024)} %param.14) | copy-start | bytes 15364
  89.6 36.6 %collective-permute-start = (bf16[1280,640]{1,0:T(8,128)(2,1)}, bf16[1280,640]{1,0:T(8,128)(2,1)}, u32[]{:S(2)}, u32[]{:S(2)}) collective-permute-start(bf16[1280,640]{1,0:T(8,128)(2,1)} %bitcast), channel_id=1, source_target_pairs={{0,1},{1,0},{2,3},{3,2},{4,5},{5,4},{6,7},{7,6},{8,9},{9,8},{10,11... | collective-permute-start | bytes 4915208 | tf_op jit(solution)/shard_map/ppermute | solution.py:100
  94.9 2.7 %copy-start.2 = (bf16[1,1,32,72,1280]{4,3,1,0,2:T(8,128)(2,1)S(1)}, bf16[1,1,32,72,1280]{4,3,1,0,2:T(8,128)(2,1)}, u32[]{:S(2)}) copy-start(bf16[1,1,32,72,1280]{4,3,1,0,2:T(8,128)(2,1)} %multiply_convert_fusion) | copy-start | bytes 17694724
  106.4 19.8 %copy-start.3 = (bf16[1,1,2,72,1280]{4,3,2,1,0:T(8,128)(2,1)S(1)}, bf16[1,1,2,72,1280]{4,3,2,1,0:T(8,128)(2,1)}, u32[]{:S(2)}) copy-start(bf16[1,1,2,72,1280]{4,3,2,1,0:T(8,128)(2,1)} %param.13) | copy-start | bytes 1105924
  106.4 19.8 %copy-start.4 = (f32[1280]{0:T(1024)S(1)}, f32[1280]{0:T(1024)}, u32[]{:S(2)}) copy-start(f32[1280]{0:T(1024)} %param.21) | copy-start | bytes 15364
  106.4 20.3 %copy-start.5 = (f32[1280]{0:T(1024)S(1)}, f32[1280]{0:T(1024)}, u32[]{:S(2)}) copy-start(f32[1280]{0:T(1024)} %param.22) | copy-start | bytes 15364
  125.5 61.2 %copy-start.8 = (f32[20]{0:T(128)S(1)}, f32[20]{0:T(128)}, u32[]{:S(2)}) copy-start(f32[20]{0:T(128)} %param.25) | copy-start | bytes 244
  183.3 11.5 %collective-permute-start.1 = (bf16[16,3,640,80]{2,3,1,0:T(8,128)(2,1)}, bf16[16,3,640,80]{2,3,1,0:T(8,128)(2,1)}, u32[]{:S(2)}, u32[]{:S(2)}) collective-permute-start(bf16[16,3,640,80]{2,3,1,0:T(8,128)(2,1)} %bitcast.95), channel_id=1, source_target_pairs={{0,1},{1,0},{2,3},{3,2},{4,5},{5,4},{6,7},{7,6},{8,9},{9,8},{10,11... | collective-permute-start | bytes 14745608 | tf_op jit(solution)/shard_map/ppermute | solution.py:136
  211.4 30.8 %copy-start.1 = (bf16[3,1280,80]{1,2,0:T(8,128)(2,1)S(1)}, bf16[3,1280,80]{1,2,0:T(8,128)(2,1)}, u32[]{:S(2)}) copy-start(bf16[3,1280,80]{1,2,0:T(8,128)(2,1)} %param.23) | copy-start | bytes 1843204
  213.1 24.3 %all-to-all-start.4 = ((bf16[16,1,9,1280]{3,2,1,0:T(8,128)(2,1)}), bf16[16,1,9,1280]{3,2,1,0:T(8,128)(2,1)S(1)}, u32[]{:S(2)}, u32[]{:S(2)}) async-start(bf16[16,1,9,1280]{3,2,1,0:T(8,128)(2,1)} %reshape.372), calls=%async_computation.4 | async-start | bytes 1310720 | tf_op jit(solution)/shard_map/all_to_all | solution.py:37
Sparse Core Ops, SparseCore 0:
  9.2 62.6 all-gather.3
  76.4 106.8 all-gather.5
